TPU v7x, 128 devices: a whole 4x4x4 slice. The times are simulated.
128 devices in a mesh: dp: 16 (over y, x_lo, core), feat: 8 (over x_hi, z).
Axes of the slice: x: 4 (x_hi: 2, x_lo: 2; x = x_hi * 2 + x_lo), y: 4, z: 4, core: 2. Of those that a mesh axis runs over, the one named last changes fastest.
Arguments:
- dataset: bfloat16 [131072, 4096], P('dp', 'feat'), may hold values from -0.09375 to 0.09375
- targets: float32 [131072], P('dp'), may hold values from 0 to 1
- indices: int32 [32768], P('dp'), may hold values from 0 to 8191
- particles: bfloat16 [1536, 4096], P('dp', 'feat'), may hold values from -6 to 6
- spread: int32 [1], replicated, may hold values from 2048 to 8191
Outputs:
- attraction: float32 [1536, 4096], P('dp', 'feat')
- repulsion: float32 [1536, 4096], P('dp', 'feat')
Inputs may be any that keep to these rules, and one draw needn't show every extreme that they name: Entry r of indices names a row within block r // 2048 of the dataset's blocks of 8192 rows.
All inputs are finite; a program needn't handle non-finite values.
Results may differ from a plain program's by a relative error of at most 0.00115.
Values may be sent and summed in bfloat16 or wider, within the bound.
No kernel may reach another device: no remote copies, remote signals or barrier semaphores. Data moves between devices by JAX's collectives and lax.ppermute only.
A program may use at most 128 MiB of HBM per device.

v0:
```python
import jax
import jax.numpy as jnp
from jax import lax
from jax.sharding import Mesh, PartitionSpec as P


DP = ("y", "xl", "c")
YX = ("y", "xl")
FT = ("xh", "z")


def contract(left, right):
    return lax.dot_general(
        left, right, (((1,), (1,)), ((), ())), preferred_element_type=jnp.float32
    )


def exact_dot(left, right):
    return jnp.dot(left, right, precision=lax.Precision.HIGHEST)


def step(dataset, targets, indices, particles, spread):
    n_feat = lax.axis_size(FT)
    batch_x = jnp.take(dataset, indices, axis=0)
    batch_t = jnp.take(targets, indices, axis=0)
    data_ratio = dataset.shape[0] / indices.shape[0]
    scale_h = spread[0].astype(jnp.float32)
    all_rows = lax.all_gather(particles, DP, axis=0, tiled=True)
    count_all = all_rows.shape[0]
    rows_own = particles.shape[0]
    inner_part = contract(particles, all_rows)
    theta_all = all_rows.astype(jnp.float32)
    sq_part = jnp.sum(theta_all * theta_all, axis=1)
    to_sum = jnp.concatenate([inner_part, sq_part[None, :]], axis=0)
    partial_t = contract(all_rows, batch_x).astype(jnp.bfloat16)
    partial_t = partial_t.reshape(n_feat, count_all // n_feat, partial_t.shape[1])
    pieces = lax.all_to_all(partial_t, FT, 0, 0, tiled=True)
    own_logits_t = jnp.sum(pieces.astype(jnp.float32), axis=0)
    own_residual_t = (batch_t[None, :] - jax.nn.sigmoid(own_logits_t)).astype(jnp.bfloat16)
    spread_res = jnp.broadcast_to(own_residual_t[None], (n_feat,) + own_residual_t.shape)
    residual_t = lax.all_to_all(spread_res, FT, 0, 0, tiled=True).reshape(count_all, -1)
    packed = lax.psum(to_sum, FT)
    inner = packed[:rows_own]
    norms_b = packed[rows_own]
    own_sq = lax.dynamic_slice_in_dim(norms_b, lax.axis_index(DP) * rows_own, rows_own, 0)
    grad_part = jnp.dot(residual_t, batch_x, preferred_element_type=jnp.float32)
    n_c = lax.axis_size("c")
    n_yx = lax.axis_size(YX)
    width = grad_part.shape[1]
    pair = lax.all_to_all(
        grad_part.reshape(n_yx, n_c, rows_own, width), "c", 1, 1, tiled=True
    )
    pair_sum = jnp.sum(pair, axis=1)
    grad_own = jnp.sum(lax.all_to_all(pair_sum, YX, 0, 0, tiled=True), axis=0)
    chips = lax.all_to_all(
        jnp.broadcast_to(grad_own[None], (n_yx,) + grad_own.shape), YX, 0, 0, tiled=True
    )
    gradient = lax.all_to_all(
        jnp.broadcast_to(chips[:, None], (n_yx, n_c, rows_own, width)), "c", 1, 1, tiled=True
    ).reshape(count_all, width)
    score = data_ratio * gradient - theta_all
    kernel = jnp.exp(-(own_sq[:, None] + norms_b[None, :] - 2.0 * inner) / scale_h)
    pushed = exact_dot(kernel, score)
    pulled = exact_dot(kernel, theta_all)
    weight = jnp.sum(kernel, axis=1)
    attraction = pushed / count_all
    repulsion = (particles.astype(jnp.float32) * weight[:, None] - pulled) / count_all
    return attraction, repulsion


def solution(mesh):
    fine = Mesh(mesh.devices.reshape(4, 2, 2, 2, 4), DP + FT)
    return jax.shard_map(
        step,
        mesh=fine,
        in_specs=(P(DP, FT), P(DP), P(DP), P(DP, FT), P()),
        out_specs=(P(DP, FT), P(DP, FT)),
        check_vma=False,
    )
```

profile of v0, /device:TPU:0, one launch (start us, length us, event | category | flops | bytes accessed | tf_op | source)
XLA Modules:
  0.0 336.4 jit_solution(17200440457011108048)
XLA Ops:
  7.2 0.0 copy-start
  7.2 0.0 all-gather.2.cloned.1.call-start
  7.2 0.7 all-gather.2.cloned.1.call-update
  7.9 0.7 fusion.11
  8.6 12.0 %gather_fusion.1 = bf16[2048,512]{1,0:T(8,128)(2,1)S(1)} fusion(bf16[8192,512]{1,0:T(8,128)(2,1)} %param.5, s32[2048]{0:T(1024)S(1)} %fusion.11), kind=kCustom, calls=%fused_computation.1 | custom fusion | bytes 4202496 | tf_op jit(solution)/shard_map/jit(_take)/gather | solution.py:24
  20.7 0.0 copy-done
  20.7 0.0 copy-start.4
  20.7 11.8 %gather_fusion = f32[2048]{0:T(1024)S(1)} fusion(f32[8192]{0:T(1024)S(1)} %copy-done, s32[2048]{0:T(1024)S(1)} %fusion.11), kind=kCustom, calls=%fused_computation | custom fusion | bytes 24576 | tf_op jit(solution)/shard_map/jit(_take)/gather | solution.py:25
  32.5 0.0 copy-done.4
  32.5 12.8 %all-gather.2.cloned.1.call-done = bf16[1536,512]{1,0:T(8,128)(2,1)} async-done(((bf16[96,512]{1,0:T(8,128)(2,1)}), bf16[1536,512]{1,0:T(8,128)(2,1)}) %all-gather.2.cloned.1.call-update) | async-done | bytes 1572880 | tf_op jit(solution)/shard_map/all_gather | solution.py:28
  45.3 5.3 %convolution_convert_fusion = bf16[2048,1536]{0,1:T(8,128)(2,1)S(1)} fusion(bf16[1536,512]{1,0:T(8,128)(2,1)} %all-gather.2.cloned.1.call-done, bf16[2048,512]{1,0:T(8,128)(2,1)S(1)} %gather_fusion.1, pred[2048]{0:T(1024)(128)(4,1)S(1)} %get-tuple-element.3), kind=kOutput, calls=%fused_computation.3 | convolution fusion | flops 3225419776 | bytes 9963520 | tf_op jit(solution)/shard_map/dot_general | solution.py:13
  50.6 79.8 %all_to_all.30 = bf16[8,192,2048]{2,1,0:T(8,128)(2,1)S(1)} all-to-all(bf16[8,192,2048]{2,1,0:T(8,128)(2,1)S(1)} %bitcast.17), channel_id=1, replica_groups=mesh['y'=4,'xl'=2,'c'=2,'xh'=2,'z'=4] {'xh','z'}, dimensions={0} | all-to-all | bytes 12582912 | tf_op jit(solution)/shard_map/all_to_all | solution.py:37
  130.4 1.2 convert_reduce_fusion
  131.6 0.4 subtract_convert_fusion
  132.0 0.8 broadcast_in_dim.47
  132.8 75.9 %all_to_all.31 = bf16[8,192,2048]{2,1,0:T(8,128)(2,1)S(1)} all-to-all(bf16[8,192,2048]{2,1,0:T(8,128)(2,1)S(1)} %broadcast_in_dim.47), channel_id=1, replica_groups=mesh['y'=4,'xl'=2,'c'=2,'xh'=2,'z'=4] {'xh','z'}, dimensions={0} | all-to-all | bytes 12582912 | tf_op jit(solution)/shard_map/all_to_all | solution.py:41
  208.7 3.5 %fusion = f32[8,2,96,512]{3,2,0,1:T(8,128)S(1)} fusion(bf16[8,2,96,2048]{3,2,1,0:T(8,128)(2,1)S(1)} %bitcast.16, bf16[2048,512]{1,0:T(8,128)(2,1)S(1)} %gather_fusion.1, pred[2048]{0:T(1024)(128)(4,1)S(1)} %get-tuple-element.3), kind=kOutput, calls=%fused_computation.4 | convolution fusion | flops 3222274048 | bytes 11536384 | tf_op jit(solution)/shard_map/dot_general | solution.py:46
  212.3 6.3 %all_to_all.32 = f32[8,2,96,512]{3,2,0,1:T(8,128)S(1)} all-to-all(f32[8,2,96,512]{3,2,0,1:T(8,128)S(1)} %fusion), channel_id=1, replica_groups=mesh['y'=4,'xl'=2,'c'=2,'xh'=2,'z'=4] {'c'}, dimensions={1} | all-to-all | bytes 6291456 | tf_op jit(solution)/shard_map/all_to_all | solution.py:50
  218.5 1.6 reduce_sum.47
  220.1 0.0 copy-start.1
  220.1 0.0 copy-start.3
  220.1 4.5 %all-to-all-start.3 = ((f32[8,96,512]{2,1,0:T(8,128)}), f32[8,96,512]{2,1,0:T(8,128)S(1)}, u32[]{:S(2)}, u32[]{:S(2)}) async-start(f32[8,96,512]{2,1,0:T(8,128)} %reduce_sum.47), calls=%async_computation.3 | async-start | bytes 3145728 | tf_op jit(solution)/shard_map/all_to_all | solution.py:54
  224.6 0.0 all-reduce.2.cloned.1.call-start
  224.6 0.0 copy-done.1
  224.7 0.4 fusion.2
  225.1 0.0 copy-done.3
  225.1 0.6 fusion.18
  225.7 0.9 pad_maximum_fusion
  226.6 0.0 all-reduce.2.cloned.1.call-update
  226.6 21.7 %all-to-all-done.3 = f32[8,96,512]{2,1,0:T(8,128)S(1)} async-done(((f32[8,96,512]{2,1,0:T(8,128)}), f32[8,96,512]{2,1,0:T(8,128)S(1)}, u32[]{:S(2)}, u32[]{:S(2)}) %all-to-all-start.3) | async-done | bytes 1572896 | tf_op jit(solution)/shard_map/all_to_all | solution.py:54
  248.3 0.1 reduce_sum.48
  248.5 1.4 broadcast_in_dim.48
  249.8 3.8 %all-to-all-start.4 = ((f32[8,96,512]{2,1,0:T(8,128)}), f32[8,96,512]{2,1,0:T(8,128)S(1)}, u32[]{:S(2)}, u32[]{:S(2)}) async-start(f32[8,96,512]{2,1,0:T(8,128)} %broadcast_in_dim.48), calls=%async_computation.4 | async-start | bytes 3145728 | tf_op jit(solution)/shard_map/all_to_all | solution.py:55
  254.2 59.5 %all-reduce.2.cloned.1.call-done = f32[97,1536]{1,0:T(8,128)} async-done(((f32[97,1536]{1,0:T(8,128)}), f32[97,1536]{1,0:T(8,128)}) %all-reduce.2.cloned.1.call-update) | async-done | bytes 595984 | tf_op jit(solution)/shard_map/psum | solution.py:42
  313.8 0.8 fusion.17
  314.6 0.1 dynamic-slice_bitcast_fusion
  314.7 1.4 fusion.15
  316.1 2.7 fusion.6
  318.8 0.0 all-to-all-done.4
  318.8 0.4 broadcast_in_dim.49
  319.2 6.3 %all_to_all.33 = f32[8,2,96,512]{3,2,0,1:T(8,128)S(1)} all-to-all(f32[8,2,96,512]{3,2,0,1:T(8,128)S(1)} %broadcast_in_dim.49), channel_id=1, replica_groups=mesh['y'=4,'xl'=2,'c'=2,'xh'=2,'z'=4] {'c'}, dimensions={1} | all-to-all | bytes 6291456 | tf_op jit(solution)/shard_map/all_to_all | solution.py:58
  325.5 0.0 copy-start.2
  325.5 0.4 copy_multiply_fusion
  325.9 0.7 copy-done.2
  326.5 3.0 fusion.5
  (2 shorter events, 0.0 us)
Async XLA Ops:
  7.2 13.5 %copy-start = (f32[8192]{0:T(1024)S(1)}, f32[8192]{0:T(1024)}, u32[]{:S(2)}) copy-start(f32[8192]{0:T(1024)} %param.6) | copy-start | bytes 98308
  7.2 38.1 %all-gather.2.cloned.1.call-start = ((), (), s32[]{:S(2)}) async-start(), calls=%async_computation.6 | async-start | bytes 1671168 | tf_op jit(solution)/shard_map/all_gather | solution.py:28
  20.7 11.8 %copy-start.4 = (s32[2048]{0:T(1024)S(1)}, s32[2048]{0:T(1024)}, u32[]{:S(2)}) copy-start(s32[2048]{0:T(1024)} %param.7) | copy-start | bytes 24580
  220.1 4.5 %copy-start.1 = (bf16[1536,512]{1,0:T(8,128)(2,1)S(1)}, bf16[1536,512]{1,0:T(8,128)(2,1)}, u32[]{:S(2)}) copy-start(bf16[1536,512]{1,0:T(8,128)(2,1)} %all-gather.2.cloned.1.call-done) | copy-start | bytes 4718596
  220.1 4.9 %copy-start.3 = (bf16[96,512]{1,0:T(8,128)(2,1)S(1)}, bf16[96,512]{1,0:T(8,128)(2,1)}, u32[]{:S(2)}) copy-start(bf16[96,512]{1,0:T(8,128)(2,1)} %param.8) | copy-start | bytes 294916
  220.1 28.2 %all-to-all-start.3 = ((f32[8,96,512]{2,1,0:T(8,128)}), f32[8,96,512]{2,1,0:T(8,128)S(1)}, u32[]{:S(2)}, u32[]{:S(2)}) async-start(f32[8,96,512]{2,1,0:T(8,128)} %reduce_sum.47), calls=%async_computation.3 | async-start | bytes 3145728 | tf_op jit(solution)/shard_map/all_to_all | solution.py:54
  224.6 89.2 %all-reduce.2.cloned.1.call-start = ((), (), s32[]{:S(2)}) async-start(), calls=%async_computation.7 | async-start | bytes 1277952 | tf_op jit(solution)/shard_map/psum | solution.py:42
  249.8 69.0 %all-to-all-start.4 = ((f32[8,96,512]{2,1,0:T(8,128)}), f32[8,96,512]{2,1,0:T(8,128)S(1)}, u32[]{:S(2)}, u32[]{:S(2)}) async-start(f32[8,96,512]{2,1,0:T(8,128)} %broadcast_in_dim.48), calls=%async_computation.4 | async-start | bytes 3145728 | tf_op jit(solution)/shard_map/all_to_all | solution.py:55
  325.5 1.1 copy-start.2
Sparse Core Ops, SparseCore 0:
  9.7 35.5 all-gather.1
  227.9 85.8 all-reduce.1
where the time goes:
time: 338 us; the launch traced here: 336 us
  blocking collectives  168 us (50%)
  waiting for transfers between devices  94.8 us (28%)
  local copies, waits for them, and re-layouts  28 us (8%)
  matrix products  15.1 us (4%)
  between operations  14.9 us (4%)
  starting transfers between devices  8.32 us (2%)
  other arithmetic  7.14 us (2%)
    all_to_all x1, blocking collectives, step(): pieces = lax.all_to_all(partial_t, FT, 0, 0, tiled=True)  79.8 us
    all_to_all x1, blocking collectives, step(): lax.all_to_all(spread_res, FT, 0, 0, tiled=True).reshape(count_all, -1)  75.9 us
    psum x1, waiting for transfers between devices, step(): packed = lax.psum(to_sum, FT)  59.5 us
    all_to_all x1, waiting for transfers between devices, step(): grad_own = jnp.sum(lax.all_to_all(pair_sum, YX, 0, 0, tiled=True), axis=0)  21.7 us
    all_gather x1, waiting for transfers between devices, step(): all_rows = lax.all_gather(particles, DP, axis=0, tiled=True)  12.8 us
    gather x1, local copies, waits for them, and re-layouts, step(): batch_x = jnp.take(dataset, indices, axis=0)  12 us
    gather x1, local copies, waits for them, and re-layouts, step(): batch_t = jnp.take(targets, indices, axis=0)  11.8 us
  transfers between devices with their start and end apart: 4, of which 3 were waited for; matrix products, arithmetic and copies ran while one was open for 10% of the time, Pallas kernels for 0%

commit v1 on v0

--- a/solution.py
+++ b/solution.py
@@ -22,10 +22,16 @@
 def step(dataset, targets, indices, particles, spread):
     n_feat = lax.axis_size(FT)
     batch_x = jnp.take(dataset, indices, axis=0)
-    batch_t = jnp.take(targets, indices, axis=0)
     data_ratio = dataset.shape[0] / indices.shape[0]
     scale_h = spread[0].astype(jnp.float32)
-    all_rows = lax.all_gather(particles, DP, axis=0, tiled=True)
+    n_c = lax.axis_size("c")
+    n_yx = lax.axis_size(YX)
+    pair_rows = lax.all_to_all(
+        jnp.broadcast_to(particles[None], (n_c,) + particles.shape), "c", 0, 0, tiled=True
+    )
+    all_rows = lax.all_to_all(
+        jnp.broadcast_to(pair_rows[None], (n_yx,) + pair_rows.shape), YX, 0, 0, tiled=True
+    ).reshape(-1, particles.shape[1])
     count_all = all_rows.shape[0]
     rows_own = particles.shape[0]
     inner_part = contract(particles, all_rows)
@@ -34,6 +40,9 @@
     to_sum = jnp.concatenate([inner_part, sq_part[None, :]], axis=0)
     partial_t = contract(all_rows, batch_x).astype(jnp.bfloat16)
     partial_t = partial_t.reshape(n_feat, count_all // n_feat, partial_t.shape[1])
+    late = lax.optimization_barrier((targets, indices, partial_t))
+    partial_t = late[2]
+    batch_t = jnp.take(late[0], late[1], axis=0)
     pieces = lax.all_to_all(partial_t, FT, 0, 0, tiled=True)
     own_logits_t = jnp.sum(pieces.astype(jnp.float32), axis=0)
     own_residual_t = (batch_t[None, :] - jax.nn.sigmoid(own_logits_t)).astype(jnp.bfloat16)
@@ -44,8 +53,6 @@
     norms_b = packed[rows_own]
     own_sq = lax.dynamic_slice_in_dim(norms_b, lax.axis_index(DP) * rows_own, rows_own, 0)
     grad_part = jnp.dot(residual_t, batch_x, preferred_element_type=jnp.float32)
-    n_c = lax.axis_size("c")
-    n_yx = lax.axis_size(YX)
     width = grad_part.shape[1]
     pair = lax.all_to_all(
         grad_part.reshape(n_yx, n_c, rows_own, width), "c", 1, 1, tiled=True

time: 338 us -> 342 us (1.012)
  blocking collectives: 168 us -> 95.6 us
  waiting for transfers between devices: 94.8 us -> 148 us
  starting transfers between devices: 8.32 us -> 20.7 us
  other arithmetic: 7.14 us -> 12 us
  local copies, waits for them, and re-layouts: 28 us -> 31.7 us
    all_to_all x1, blocking collectives: 79.8 us -> 3.89 us  [step(): lax.all_to_all(jnp.broadcast_to(particles[None], (n_c,) + particles.shape...]
    all_to_all x0 -> x2, waiting for transfers between devices: none -> 66.8 us  [the longest x1 58.8 us: step(): pieces = lax.all_to_all(partial_t, FT, 0, 0, tiled=True)]
    all_to_all x0 -> x2, starting transfers between devices: none -> 13 us  [the longest x1 7.47 us: step(): pieces = lax.all_to_all(partial_t, FT, 0, 0, tiled=True)]
    all_gather x1 -> x0, waiting for transfers between devices: 12.8 us -> none  [step(): all_rows = lax.all_gather(particles, DP, axis=0, tiled=True)]
  transfers between devices with their start and end apart: 4 -> 5, of which waited for: 3 -> 4; matrix products, arithmetic and copies ran while one was open for 10% -> 10% of each run, Pallas kernels for 0% -> 0%
where the time goes in v1:
time: 342 us; the launch traced here: 340 us
  waiting for transfers between devices  148 us (43%)
  blocking collectives  95.6 us (28%)
  local copies, waits for them, and re-layouts  31.7 us (9%)
  starting transfers between devices  20.7 us (6%)
  matrix products  17.4 us (5%)
  between operations  14.8 us (4%)
  other arithmetic  12 us (4%)
    all_to_all x1, blocking collectives, step(): lax.all_to_all(spread_res, FT, 0, 0, tiled=True).reshape(count_all, -1)  78.2 us
    psum x1, waiting for transfers between devices, step(): packed = lax.psum(to_sum, FT)  59.5 us
    all_to_all x1, waiting for transfers between devices, step(): pieces = lax.all_to_all(partial_t, FT, 0, 0, tiled=True)  58.8 us
    all_to_all x1, waiting for transfers between devices, step(): grad_own = jnp.sum(lax.all_to_all(pair_sum, YX, 0, 0, tiled=True), axis=0)  21.7 us
    gather x1, local copies, waits for them, and re-layouts, step(): batch_x = jnp.take(dataset, indices, axis=0)  13.7 us
    gather x1, local copies, waits for them, and re-layouts, step(): batch_t = jnp.take(late[0], late[1], axis=0)  11.8 us
    dot_general x2, matrix products, contract(): lax.dot_general(left, right, (((1,), (1,)), ((), ())), preferred_element_...  8.39 us
    all_to_all x1, waiting for transfers between devices, step(): lax.all_to_all(jnp.broadcast_to(pair_rows[None], (n_yx,) + pair_rows.shap...  7.95 us
  transfers between devices with their start and end apart: 5, of which 4 were waited for; matrix products, arithmetic and copies ran while one was open for 10% of the time, Pallas kernels for 0%

profile of v1, /device:TPU:0, one launch (start us, length us, event | category | flops | bytes accessed | tf_op | source)
XLA Modules:
  0.0 340.3 jit_solution(16278915059833481897)
XLA Ops:
  7.2 0.0 copy-start
  7.2 0.9 broadcast_in_dim.32
  8.1 3.9 %all_to_all.40 = bf16[2,96,512]{2,1,0:T(8,128)(2,1)S(1)} all-to-all(bf16[2,96,512]{2,1,0:T(8,128)(2,1)S(1)} %broadcast_in_dim.32), channel_id=1, replica_groups=mesh['y'=4,'xl'=2,'c'=2,'xh'=2,'z'=4] {'c'}, dimensions={0} | all-to-all | bytes 393216 | tf_op jit(solution)/shard_map/all_to_all | solution.py:29
  12.0 1.3 broadcast_in_dim.33
  13.3 5.5 %all-to-all-start.1 = ((bf16[8,2,96,512]{3,2,1,0:T(8,128)(2,1)}), bf16[8,2,96,512]{3,2,1,0:T(8,128)(2,1)S(1)}, u32[]{:S(2)}, u32[]{:S(2)}) async-start(bf16[8,2,96,512]{3,2,1,0:T(8,128)(2,1)} %broadcast_in_dim.33), calls=%async_computation.1 | async-start | bytes 3145728 | tf_op jit(solution)/shard_map/all_to_all | solution.py:32
  18.8 0.0 copy-done.5
  18.8 13.7 %gather_fusion = bf16[2048,512]{1,0:T(8,128)(2,1)} fusion(bf16[8192,512]{1,0:T(8,128)(2,1)} %param.5, s32[2048]{0:T(1024)S(1)} %fusion.8), kind=kCustom, calls=%fused_computation | custom fusion | bytes 4202496 | tf_op jit(solution)/shard_map/jit(_take)/gather | solution.py:24
  32.5 8.0 %all-to-all-done.1 = bf16[8,2,96,512]{3,2,1,0:T(8,128)(2,1)S(1)} async-done(((bf16[8,2,96,512]{3,2,1,0:T(8,128)(2,1)}), bf16[8,2,96,512]{3,2,1,0:T(8,128)(2,1)S(1)}, u32[]{:S(2)}, u32[]{:S(2)}) %all-to-all-start.1) | async-done | bytes 1572896 | tf_op jit(solution)/shard_map/all_to_all | solution.py:32
  40.5 7.8 %convolution_convert_fusion = bf16[2048,1536]{0,1:T(8,128)(2,1)} fusion(bf16[1536,512]{1,0:T(8,128)(2,1)S(1)} %bitcast.19, bf16[2048,512]{1,0:T(8,128)(2,1)} %gather_fusion, pred[2048]{0:T(1024)(128)(4,1)S(1)} %compare_and_fusion), kind=kOutput, calls=%fused_computation.3 | convolution fusion | flops 3225419776 | bytes 9963520 | tf_op jit(solution)/shard_map/dot_general | solution.py:13
  48.3 7.5 %all-to-all-start.2 = ((bf16[8,192,2048]{2,1,0:T(8,128)(2,1)}), bf16[8,192,2048]{2,1,0:T(8,128)(2,1)}, u32[]{:S(2)}, u32[]{:S(2)}) async-start(bf16[8,192,2048]{2,1,0:T(8,128)(2,1)} %bitcast.22), calls=%async_computation.2 | async-start | bytes 12582912 | tf_op jit(solution)/shard_map/all_to_all | solution.py:46
  55.8 0.0 copy-done
  55.8 11.8 %gather_fusion.1 = f32[2048]{0:T(1024)S(1)} fusion(f32[8192]{0:T(1024)S(1)} %copy-done, s32[2048]{0:T(1024)S(1)} %fusion.9), kind=kCustom, calls=%fused_computation.1 | custom fusion | bytes 24576 | tf_op jit(solution)/shard_map/jit(_take)/gather | solution.py:45
  67.6 58.8 %all-to-all-done.2 = bf16[8,192,2048]{2,1,0:T(8,128)(2,1)} async-done(((bf16[8,192,2048]{2,1,0:T(8,128)(2,1)}), bf16[8,192,2048]{2,1,0:T(8,128)(2,1)}, u32[]{:S(2)}, u32[]{:S(2)}) %all-to-all-start.2) | async-done | bytes 6291488 | tf_op jit(solution)/shard_map/all_to_all | solution.py:46
  126.4 4.2 %convert_reduce_fusion = f32[192,2048]{1,0:T(8,128)S(1)} fusion(bf16[8,192,2048]{2,1,0:T(8,128)(2,1)} %all-to-all-done.2), kind=kLoop, calls=%fused_computation.2 | loop fusion | flops 5898240 | bytes 7864320 | tf_op jit(solution)/shard_map/reduce_sum | solution.py:47
  130.6 0.4 subtract_convert_fusion
  131.0 0.8 broadcast_in_dim.64
  131.8 0.0 copy-start.3
  131.8 78.2 %all_to_all.41 = bf16[8,192,2048]{2,1,0:T(8,128)(2,1)S(1)} all-to-all(bf16[8,192,2048]{2,1,0:T(8,128)(2,1)S(1)} %broadcast_in_dim.64), channel_id=1, replica_groups=mesh['y'=4,'xl'=2,'c'=2,'xh'=2,'z'=4] {'xh','z'}, dimensions={0} | all-to-all | bytes 12582912 | tf_op jit(solution)/shard_map/all_to_all | solution.py:50
  210.0 0.0 copy-done.3
  210.0 3.5 %fusion = f32[8,2,96,512]{3,2,0,1:T(8,128)S(1)} fusion(bf16[8,2,96,2048]{3,2,1,0:T(8,128)(2,1)S(1)} %bitcast.23, bf16[2048,512]{1,0:T(8,128)(2,1)S(1)} %copy-done.3, pred[2048]{0:T(1024)(128)(4,1)S(1)} %compare_and_fusion), kind=kOutput, calls=%fused_computation.4 | convolution fusion | flops 3222274048 | bytes 11536384 | tf_op jit(solution)/shard_map/dot_general | solution.py:55
  213.5 7.2 %all_to_all.42 = f32[8,2,96,512]{3,2,0,1:T(8,128)} all-to-all(f32[8,2,96,512]{3,2,0,1:T(8,128)S(1)} %fusion), channel_id=1, replica_groups=mesh['y'=4,'xl'=2,'c'=2,'xh'=2,'z'=4] {'c'}, dimensions={1} | all-to-all | bytes 6291456 | tf_op jit(solution)/shard_map/all_to_all | solution.py:57
  220.8 3.5 %reduce_sum.47 = f32[8,96,512]{2,1,0:T(8,128)} reduce(f32[8,2,96,512]{3,2,0,1:T(8,128)} %all_to_all.42, f32[]{:T(128)} %constant.27.clone.1), dimensions={1}, to_apply=%region_3.4 | reduce | flops 393216 | bytes 4718596 | tf_op jit(solution)/shard_map/reduce_sum | solution.py:60
  224.3 4.1 %all-to-all-start.5 = ((f32[8,96,512]{2,1,0:T(8,128)}), f32[8,96,512]{2,1,0:T(8,128)S(1)}, u32[]{:S(2)}, u32[]{:S(2)}) async-start(f32[8,96,512]{2,1,0:T(8,128)} %reduce_sum.47), calls=%async_computation.5 | async-start | bytes 3145728 | tf_op jit(solution)/shard_map/all_to_all | solution.py:61
  228.4 0.0 all-reduce.2.cloned.1.call-start
  228.5 0.4 multiply_reduce_fusion
  228.9 0.1 broadcast_in_dim.58
  229.0 0.6 fusion.16
  229.6 0.9 pad_maximum_fusion
  230.5 0.0 all-reduce.2.cloned.1.call-update
  230.5 21.7 %all-to-all-done.5 = f32[8,96,512]{2,1,0:T(8,128)S(1)} async-done(((f32[8,96,512]{2,1,0:T(8,128)}), f32[8,96,512]{2,1,0:T(8,128)S(1)}, u32[]{:S(2)}, u32[]{:S(2)}) %all-to-all-start.5) | async-done | bytes 1572896 | tf_op jit(solution)/shard_map/all_to_all | solution.py:61
  252.2 0.1 reduce_sum.48
  252.4 1.4 broadcast_in_dim.65
  253.7 3.6 %all-to-all-start.6 = ((f32[8,96,512]{2,1,0:T(8,128)}), f32[8,96,512]{2,1,0:T(8,128)S(1)}, u32[]{:S(2)}, u32[]{:S(2)}) async-start(f32[8,96,512]{2,1,0:T(8,128)} %broadcast_in_dim.65), calls=%async_computation.6 | async-start | bytes 3145728 | tf_op jit(solution)/shard_map/all_to_all | solution.py:62
  258.0 59.5 %all-reduce.2.cloned.1.call-done = f32[97,1536]{1,0:T(8,128)} async-done(((f32[97,1536]{1,0:T(8,128)}), f32[97,1536]{1,0:T(8,128)}) %all-reduce.2.cloned.1.call-update) | async-done | bytes 595984 | tf_op jit(solution)/shard_map/psum | solution.py:51
  317.5 0.8 fusion.15
  318.3 0.1 dynamic-slice_bitcast_fusion
  318.4 1.4 fusion.13
  319.8 2.7 fusion.3
  322.5 0.0 all-to-all-done.6
  322.5 0.4 broadcast_in_dim.66
  322.9 6.3 %all_to_all.43 = f32[8,2,96,512]{3,2,0,1:T(8,128)S(1)} all-to-all(f32[8,2,96,512]{3,2,0,1:T(8,128)S(1)} %broadcast_in_dim.66), channel_id=1, replica_groups=mesh['y'=4,'xl'=2,'c'=2,'xh'=2,'z'=4] {'c'}, dimensions={1} | all-to-all | bytes 6291456 | tf_op jit(solution)/shard_map/all_to_all | solution.py:65
  329.2 0.4 copy_multiply_fusion
  329.6 0.0 copy-start.2
  329.6 0.0 copy-start.1
  329.6 0.6 bitcast_subtract_fusion
  330.2 0.4 copy-done.2
  330.7 2.8 convolution_multiply_fusion
  333.5 0.0 copy-done.1
  (7 shorter events, 0.0 us)
Async XLA Ops:
  7.2 48.6 %copy-start = (f32[8192]{0:T(1024)S(1)}, f32[8192]{0:T(1024)}, u32[]{:S(2)}) copy-start(f32[8192]{0:T(1024)} %param.6) | copy-start | bytes 98308
  12.0 6.8 %copy-start.5 = (s32[2048]{0:T(1024)S(1)}, s32[2048]{0:T(1024)}, u32[]{:S(2)}) copy-start(s32[2048]{0:T(1024)} %param.7) | copy-start | bytes 24580
  13.3 27.2 %all-to-all-start.1 = ((bf16[8,2,96,512]{3,2,1,0:T(8,128)(2,1)}), bf16[8,2,96,512]{3,2,1,0:T(8,128)(2,1)S(1)}, u32[]{:S(2)}, u32[]{:S(2)}) async-start(bf16[8,2,96,512]{3,2,1,0:T(8,128)(2,1)} %broadcast_in_dim.33), calls=%async_computation.1 | async-start | bytes 3145728 | tf_op jit(solution)/shard_map/all_to_all | solution.py:32
  48.3 78.1 %all-to-all-start.2 = ((bf16[8,192,2048]{2,1,0:T(8,128)(2,1)}), bf16[8,192,2048]{2,1,0:T(8,128)(2,1)}, u32[]{:S(2)}, u32[]{:S(2)}) async-start(bf16[8,192,2048]{2,1,0:T(8,128)(2,1)} %bitcast.22), calls=%async_computation.2 | async-start | bytes 12582912 | tf_op jit(solution)/shard_map/all_to_all | solution.py:46
  131.8 78.2 %copy-start.3 = (bf16[2048,512]{1,0:T(8,128)(2,1)S(1)}, bf16[2048,512]{1,0:T(8,128)(2,1)}, u32[]{:S(2)}) copy-start(bf16[2048,512]{1,0:T(8,128)(2,1)} %gather_fusion) | copy-start | bytes 6291460
  224.3 4.7 %copy-start.4 = (bf16[96,512]{1,0:T(8,128)(2,1)S(1)}, bf16[96,512]{1,0:T(8,128)(2,1)}, u32[]{:S(2)}) copy-start(bf16[96,512]{1,0:T(8,128)(2,1)} %param.8) | copy-start | bytes 294916
  224.3 28.0 %all-to-all-start.5 = ((f32[8,96,512]{2,1,0:T(8,128)}), f32[8,96,512]{2,1,0:T(8,128)S(1)}, u32[]{:S(2)}, u32[]{:S(2)}) async-start(f32[8,96,512]{2,1,0:T(8,128)} %reduce_sum.47), calls=%async_computation.5 | async-start | bytes 3145728 | tf_op jit(solution)/shard_map/all_to_all | solution.py:61
  228.4 89.1 %all-reduce.2.cloned.1.call-start = ((), (), s32[]{:S(2)}) async-start(), calls=%async_computation.8 | async-start | bytes 1277952 | tf_op jit(solution)/shard_map/psum | solution.py:51
  253.7 68.8 %all-to-all-start.6 = ((f32[8,96,512]{2,1,0:T(8,128)}), f32[8,96,512]{2,1,0:T(8,128)S(1)}, u32[]{:S(2)}, u32[]{:S(2)}) async-start(f32[8,96,512]{2,1,0:T(8,128)} %broadcast_in_dim.65), calls=%async_computation.6 | async-start | bytes 3145728 | tf_op jit(solution)/shard_map/all_to_all | solution.py:62
  329.6 1.1 copy-start.2
  329.6 3.9 %copy-start.1 = (f32[8192]{0:T(1024)S(1)}, f32[8192]{0:T(1024)}, u32[]{:S(2)}) copy-start(f32[8192]{0:T(1024)} %param.6) | copy-start | bytes 98308
Sparse Core Ops, SparseCore 0:
  231.7 85.7 all-reduce.1

commit v2 on v1

--- a/solution.py
+++ b/solution.py
@@ -38,6 +38,15 @@
     theta_all = all_rows.astype(jnp.float32)
     sq_part = jnp.sum(theta_all * theta_all, axis=1)
     to_sum = jnp.concatenate([inner_part, sq_part[None, :]], axis=0)
+    per_peer = -(-to_sum.shape[0] // n_feat)
+    to_sum = jnp.pad(to_sum, ((0, per_peer * n_feat - to_sum.shape[0]), (0, 0)))
+    me = lax.axis_index(FT)
+    inner_own = lax.dynamic_slice_in_dim(to_sum, me * per_peer, per_peer, 0)
+    for k in range(1, n_feat):
+        piece = lax.dynamic_slice_in_dim(to_sum, ((me + k) % n_feat) * per_peer, per_peer, 0)
+        inner_own = inner_own + lax.ppermute(
+            piece, FT, [(i, (i + k) % n_feat) for i in range(n_feat)]
+        )
     partial_t = contract(all_rows, batch_x).astype(jnp.bfloat16)
     partial_t = partial_t.reshape(n_feat, count_all // n_feat, partial_t.shape[1])
     late = lax.optimization_barrier((targets, indices, partial_t))
@@ -48,7 +57,12 @@
     own_residual_t = (batch_t[None, :] - jax.nn.sigmoid(own_logits_t)).astype(jnp.bfloat16)
     spread_res = jnp.broadcast_to(own_residual_t[None], (n_feat,) + own_residual_t.shape)
     residual_t = lax.all_to_all(spread_res, FT, 0, 0, tiled=True).reshape(count_all, -1)
-    packed = lax.psum(to_sum, FT)
+    got = [inner_own] + [
+        lax.ppermute(inner_own, FT, [(i, (i + k) % n_feat) for i in range(n_feat)])
+        for k in range(1, n_feat)
+    ]
+    order = (me - jnp.arange(n_feat)) % n_feat
+    packed = jnp.take(jnp.stack(got), order, axis=0).reshape(-1, count_all)
     inner = packed[:rows_own]
     norms_b = packed[rows_own]
     own_sq = lax.dynamic_slice_in_dim(norms_b, lax.axis_index(DP) * rows_own, rows_own, 0)

time: 342 us -> 322 us (0.942)
  blocking collectives: 95.6 us -> 17.4 us
  starting transfers between devices: 20.7 us -> 61.1 us
  local copies, waits for them, and re-layouts: 31.7 us -> 46.1 us
  waiting for transfers between devices: 148 us -> 162 us
  between operations: 14.8 us -> 1.64 us
    all_to_all x1 -> x0, blocking collectives: 78.2 us -> none  [step(): lax.all_to_all(spread_res, FT, 0, 0, tiled=True).reshape(count_all, -1)]
    ppermute x0 -> x14, waiting for transfers between devices: none -> 66.2 us  [the longest x7 66.2 us: step(): lax.ppermute(piece, FT, [(i, (i + k) % n_feat) for i in range(n_feat)])]
    psum x1 -> x0, waiting for transfers between devices: 59.5 us -> none  [step(): packed = lax.psum(to_sum, FT)]
    ppermute x0 -> x14, starting transfers between devices: none -> 36 us  [the longest x7 20.3 us: step(): lax.ppermute(inner_own, FT, [(i, (i + k) % n_feat) for i in range(n_feat)])]
    all_to_all x1, waiting for transfers between devices: 0.01 us -> 11.1 us  [step(): lax.all_to_all(jnp.broadcast_to(grad_own[None], (n_yx,) + grad_own.shape)...]
    unnamed x12 -> x18, local copies, waits for them, and re-layouts: 0.48 us -> 6.52 us
    all_to_all x0 -> x1, starting transfers between devices: none -> 4.9 us  [step(): lax.all_to_all(spread_res, FT, 0, 0, tiled=True).reshape(count_all, -1)]
    gather x0 -> x2, local copies, waits for them, and re-layouts: none -> 4.68 us  [step(): packed = jnp.take(jnp.stack(got), order, axis=0).reshape(-1, count_all)]
  transfers between devices with their start and end apart: 5 -> 19, of which waited for: 4 -> 9; matrix products, arithmetic and copies ran while one was open for 10% -> 17% of each run, Pallas kernels for 0% -> 0%
where the time goes in v2:
time: 322 us; the launch traced here: 320 us
  waiting for transfers between devices  162 us (50%)
  starting transfers between devices  61.1 us (19%)
  local copies, waits for them, and re-layouts  46.1 us (14%)
  matrix products  19.8 us (6%)
  blocking collectives  17.4 us (5%)
  other arithmetic  12 us (4%)
    ppermute x7, waiting for transfers between devices, step(): lax.ppermute(piece, FT, [(i, (i + k) % n_feat) for i in range(n_feat)])  66.2 us
    all_to_all x1, waiting for transfers between devices, step(): pieces = lax.all_to_all(partial_t, FT, 0, 0, tiled=True)  58.8 us
    ppermute x7, starting transfers between devices, step(): lax.ppermute(inner_own, FT, [(i, (i + k) % n_feat) for i in range(n_feat)])  20.3 us
    all_to_all x1, waiting for transfers between devices, step(): grad_own = jnp.sum(lax.all_to_all(pair_sum, YX, 0, 0, tiled=True), axis=0)  17.5 us
    ppermute x7, starting transfers between devices, step(): lax.ppermute(piece, FT, [(i, (i + k) % n_feat) for i in range(n_feat)])  15.8 us
    gather x1, local copies, waits for them, and re-layouts, step(): batch_x = jnp.take(dataset, indices, axis=0)  13.7 us
    gather x1, local copies, waits for them, and re-layouts, step(): batch_t = jnp.take(late[0], late[1], axis=0)  11.8 us
    all_to_all x1, waiting for transfers between devices, step(): lax.all_to_all(jnp.broadcast_to(grad_own[None], (n_yx,) + grad_own.shape)...  11.1 us
  transfers between devices with their start and end apart: 19, of which 9 were waited for; matrix products, arithmetic and copies ran while one was open for 17% of the time, Pallas kernels for 0%

profile of v2, /device:TPU:0, one launch (start us, length us, event | category | flops | bytes accessed | tf_op | source)
XLA Modules:
  0.0 319.6 jit_solution(16077233212510317907)
XLA Ops:
  0.6 0.9 broadcast_in_dim.73
  1.6 3.9 %all_to_all.40 = bf16[2,96,512]{2,1,0:T(8,128)(2,1)S(1)} all-to-all(bf16[2,96,512]{2,1,0:T(8,128)(2,1)S(1)} %broadcast_in_dim.73), channel_id=1, replica_groups=mesh['y'=4,'xl'=2,'c'=2,'xh'=2,'z'=4] {'c'}, dimensions={0} | all-to-all | bytes 393216 | tf_op jit(solution)/shard_map/all_to_all | solution.py:29
  5.5 1.3 broadcast_in_dim.74
  6.8 5.5 %all-to-all-start.1 = ((bf16[8,2,96,512]{3,2,1,0:T(8,128)(2,1)}), bf16[8,2,96,512]{3,2,1,0:T(8,128)(2,1)S(1)}, u32[]{:S(2)}, u32[]{:S(2)}) async-start(bf16[8,2,96,512]{3,2,1,0:T(8,128)(2,1)} %broadcast_in_dim.74), calls=%async_computation.1 | async-start | bytes 3145728 | tf_op jit(solution)/shard_map/all_to_all | solution.py:32
  12.3 13.7 %gather_fusion.1 = bf16[2048,512]{1,0:T(8,128)(2,1)} fusion(bf16[8192,512]{1,0:T(8,128)(2,1)} %param.5, s32[2048]{0:T(1024)S(1)} %fusion.8), kind=kCustom, calls=%fused_computation.1 | custom fusion | bytes 4202496 | tf_op jit(solution)/shard_map/jit(_take)/gather | solution.py:24
  26.0 8.0 %all-to-all-done.1 = bf16[8,2,96,512]{3,2,1,0:T(8,128)(2,1)S(1)} async-done(((bf16[8,2,96,512]{3,2,1,0:T(8,128)(2,1)}), bf16[8,2,96,512]{3,2,1,0:T(8,128)(2,1)S(1)}, u32[]{:S(2)}, u32[]{:S(2)}) %all-to-all-start.1) | async-done | bytes 1572896 | tf_op jit(solution)/shard_map/all_to_all | solution.py:32
  34.0 7.8 %convolution_convert_fusion = bf16[2048,1536]{0,1:T(8,128)(2,1)} fusion(bf16[1536,512]{1,0:T(8,128)(2,1)S(1)} %bitcast.37, bf16[2048,512]{1,0:T(8,128)(2,1)} %gather_fusion.1, pred[2048]{0:T(1024)(128)(4,1)S(1)} %compare_and_fusion), kind=kOutput, calls=%fused_computation.4 | convolution fusion | flops 3225419776 | bytes 9963520 | tf_op jit(solution)/shard_map/dot_general | solution.py:13
  41.7 7.5 %all-to-all-start.2 = ((bf16[8,192,2048]{2,1,0:T(8,128)(2,1)}), bf16[8,192,2048]{2,1,0:T(8,128)(2,1)}, u32[]{:S(2)}, u32[]{:S(2)}) async-start(bf16[8,192,2048]{2,1,0:T(8,128)(2,1)} %bitcast.40), calls=%async_computation.2 | async-start | bytes 12582912 | tf_op jit(solution)/shard_map/all_to_all | solution.py:55
  49.2 11.8 %gather_fusion.2 = f32[2048]{0:T(1024)S(1)} fusion(f32[8192]{0:T(1024)S(1)} %copy-done, s32[2048]{0:T(1024)S(1)} %fusion.9), kind=kCustom, calls=%fused_computation.2 | custom fusion | bytes 24576 | tf_op jit(solution)/shard_map/jit(_take)/gather | solution.py:54
  61.0 58.8 %all-to-all-done.2 = bf16[8,192,2048]{2,1,0:T(8,128)(2,1)} async-done(((bf16[8,192,2048]{2,1,0:T(8,128)(2,1)}), bf16[8,192,2048]{2,1,0:T(8,128)(2,1)}, u32[]{:S(2)}, u32[]{:S(2)}) %all-to-all-start.2) | async-done | bytes 6291488 | tf_op jit(solution)/shard_map/all_to_all | solution.py:55
  119.9 4.2 %convert_reduce_fusion = f32[192,2048]{1,0:T(8,128)S(1)} fusion(bf16[8,192,2048]{2,1,0:T(8,128)(2,1)} %all-to-all-done.2), kind=kLoop, calls=%fused_computation.3 | loop fusion | flops 5898240 | bytes 7864320 | tf_op jit(solution)/shard_map/reduce_sum | solution.py:56
  124.5 3.5 %broadcast_in_dim.82 = bf16[8,192,2048]{2,1,0:T(8,128)(2,1)} broadcast(bf16[192,2048]{1,0:T(8,128)(2,1)S(1)} %subtract_convert_fusion), dimensions={1,2} | broadcast | bytes 7077888 | tf_op jit(solution)/shard_map/broadcast_in_dim | solution.py:58
  127.9 4.9 %all-to-all-start.3 = ((bf16[8,192,2048]{2,1,0:T(8,128)(2,1)}), bf16[8,192,2048]{2,1,0:T(8,128)(2,1)}, u32[]{:S(2)}, u32[]{:S(2)}) async-start(bf16[8,192,2048]{2,1,0:T(8,128)(2,1)} %broadcast_in_dim.82), calls=%async_computation.3 | async-start | bytes 12582912 | tf_op jit(solution)/shard_map/all_to_all | solution.py:59
  134.2 5.6 %collective-permute-start.6 = (f32[13,1536]{1,0:T(8,128)S(1)}, f32[13,1536]{1,0:T(8,128)S(1)}, u32[]{:S(2)}, u32[]{:S(2)}) collective-permute-start(f32[13,1536]{1,0:T(8,128)S(1)} %get-tuple-element.18), channel_id=1, source_target_pairs={{0,7},{1,0},{2,1},{3,2},{4,3},{5,4},{6,5},{7,6},{8,15},{9,8},{10,9... | collective-permute-start | bytes 239624 | tf_op jit(solution)/shard_map/ppermute | solution.py:47
  139.8 0.9 collective-permute-start.5
  141.5 0.9 collective-permute-start.4
  142.4 3.0 collective-permute-start.3
  145.4 60.4 %collective-permute-done.6 = f32[13,1536]{1,0:T(8,128)S(1)} collective-permute-done((f32[13,1536]{1,0:T(8,128)S(1)}, f32[13,1536]{1,0:T(8,128)S(1)}, u32[]{:S(2)}, u32[]{:S(2)}) %collective-permute-start.6) | collective-permute-done | bytes 79904 | tf_op jit(solution)/shard_map/ppermute | solution.py:47
  205.8 2.8 collective-permute-start.1
  208.7 2.6 collective-permute-start
  211.3 1.5 collective-permute-done.3
  212.8 1.0 collective-permute-done.2
  213.8 1.9 collective-permute-done.1
  215.7 1.4 collective-permute-done
  217.1 0.7 bitcast_dynamic-update-slice_fusion.7
  217.8 1.2 collective-permute-start.7
  219.0 2.6 collective-permute-start.8
  221.7 5.6 %collective-permute-start.9 = (f32[13,1536]{1,0:T(8,128)}, f32[13,1536]{1,0:T(8,128)}, u32[]{:S(2)}, u32[]{:S(2)}) collective-permute-start(f32[13,1536]{1,0:T(8,128)} %get-tuple-element.9), channel_id=1, source_target_pairs={{0,3},{1,4},{2,5},{3,6},{4,7},{5,0},{6,1},{7,2},{8,11},{9,12},{10,... | collective-permute-start | bytes 239624 | tf_op jit(solution)/shard_map/ppermute | solution.py:61
  227.2 3.8 %collective-permute-start.11 = (f32[13,1536]{1,0:T(8,128)}, f32[13,1536]{1,0:T(8,128)S(1)}, u32[]{:S(2)}, u32[]{:S(2)}) collective-permute-start(f32[13,1536]{1,0:T(8,128)} %get-tuple-element.9), channel_id=1, source_target_pairs={{0,5},{1,6},{2,7},{3,0},{4,1},{5,2},{6,3},{7,4},{8,13},{9,14},{10,... | collective-permute-start | bytes 239624 | tf_op jit(solution)/shard_map/ppermute | solution.py:61
  231.0 3.9 %collective-permute-start.12 = (f32[13,1536]{1,0:T(8,128)}, f32[13,1536]{1,0:T(8,128)S(1)}, u32[]{:S(2)}, u32[]{:S(2)}) collective-permute-start(f32[13,1536]{1,0:T(8,128)} %get-tuple-element.9), channel_id=1, source_target_pairs={{0,6},{1,7},{2,0},{3,1},{4,2},{5,3},{6,4},{7,5},{8,14},{9,15},{10,... | collective-permute-start | bytes 239624 | tf_op jit(solution)/shard_map/ppermute | solution.py:61
  235.6 3.2 collective-permute-start.13
  239.4 7.0 %fusion = f32[8,2,96,512]{3,2,0,1:T(8,128)S(1)} fusion(bf16[8,2,96,2048]{3,2,1,0:T(8,128)(2,1)} %bitcast.14, bf16[2048,512]{1,0:T(8,128)(2,1)} %gather_fusion.1, pred[2048]{0:T(1024)(128)(4,1)S(1)} %compare_and_fusion), kind=kOutput, calls=%fused_computation.5 | convolution fusion | flops 3222274048 | bytes 11536384 | tf_op jit(solution)/shard_map/dot_general | solution.py:69
  246.4 7.2 %all_to_all.41 = f32[8,2,96,512]{3,2,0,1:T(8,128)} all-to-all(f32[8,2,96,512]{3,2,0,1:T(8,128)S(1)} %fusion), channel_id=1, replica_groups=mesh['y'=4,'xl'=2,'c'=2,'xh'=2,'z'=4] {'c'}, dimensions={1} | all-to-all | bytes 6291456 | tf_op jit(solution)/shard_map/all_to_all | solution.py:71
  253.6 3.5 %reduce_sum.47 = f32[8,96,512]{2,1,0:T(8,128)} reduce(f32[8,2,96,512]{3,2,0,1:T(8,128)} %all_to_all.41, f32[]{:T(128)} %constant.123.clone.1), dimensions={1}, to_apply=%region_2.3 | reduce | flops 393216 | bytes 4718596 | tf_op jit(solution)/shard_map/reduce_sum | solution.py:74
  257.1 3.6 %all-to-all-start.5 = ((f32[8,96,512]{2,1,0:T(8,128)}), f32[8,96,512]{2,1,0:T(8,128)S(1)}, u32[]{:S(2)}, u32[]{:S(2)}) async-start(f32[8,96,512]{2,1,0:T(8,128)} %reduce_sum.47), calls=%async_computation.5 | async-start | bytes 3145728 | tf_op jit(solution)/shard_map/all_to_all | solution.py:75
  260.7 1.5 bitcast_dynamic-update-slice_fusion.4
  262.3 1.5 bitcast_dynamic-update-slice_fusion.3
  265.1 17.5 %all-to-all-done.5 = f32[8,96,512]{2,1,0:T(8,128)S(1)} async-done(((f32[8,96,512]{2,1,0:T(8,128)}), f32[8,96,512]{2,1,0:T(8,128)S(1)}, u32[]{:S(2)}, u32[]{:S(2)}) %all-to-all-start.5) | async-done | bytes 1572896 | tf_op jit(solution)/shard_map/all_to_all | solution.py:75
  282.7 1.4 broadcast_in_dim.83
  284.1 3.6 %all-to-all-start.6 = ((f32[8,96,512]{2,1,0:T(8,128)}), f32[8,96,512]{2,1,0:T(8,128)S(1)}, u32[]{:S(2)}, u32[]{:S(2)}) async-start(f32[8,96,512]{2,1,0:T(8,128)} %broadcast_in_dim.83), calls=%async_computation.6 | async-start | bytes 3145728 | tf_op jit(solution)/shard_map/all_to_all | solution.py:76
  287.7 1.5 bitcast_dynamic-update-slice_fusion
  289.2 2.6 gather_fusion
  291.9 2.1 gather.15
  293.9 1.2 broadcast_select_fusion.3
  296.0 1.7 fusion.3
  297.6 11.1 %all-to-all-done.6 = f32[8,96,512]{2,1,0:T(8,128)S(1)} async-done(((f32[8,96,512]{2,1,0:T(8,128)}), f32[8,96,512]{2,1,0:T(8,128)S(1)}, u32[]{:S(2)}, u32[]{:S(2)}) %all-to-all-start.6) | async-done | bytes 1572896 | tf_op jit(solution)/shard_map/all_to_all | solution.py:76
  309.1 6.3 %all_to_all.42 = f32[8,2,96,512]{3,2,0,1:T(8,128)S(1)} all-to-all(f32[8,2,96,512]{3,2,0,1:T(8,128)S(1)} %broadcast_in_dim.84), channel_id=1, replica_groups=mesh['y'=4,'xl'=2,'c'=2,'xh'=2,'z'=4] {'c'}, dimensions={1} | all-to-all | bytes 6291456 | tf_op jit(solution)/shard_map/all_to_all | solution.py:79
  316.9 2.8 convolution_multiply_fusion
  (50 shorter events, 7.3 us)
Async XLA Ops:
  0.6 48.6 %copy-start = (f32[8192]{0:T(1024)S(1)}, f32[8192]{0:T(1024)}, u32[]{:S(2)}) copy-start(f32[8192]{0:T(1024)} %param.6) | copy-start | bytes 98308
  5.5 6.8 %copy-start.5 = (s32[2048]{0:T(1024)S(1)}, s32[2048]{0:T(1024)}, u32[]{:S(2)}) copy-start(s32[2048]{0:T(1024)} %param.7) | copy-start | bytes 24580
  6.8 27.2 %all-to-all-start.1 = ((bf16[8,2,96,512]{3,2,1,0:T(8,128)(2,1)}), bf16[8,2,96,512]{3,2,1,0:T(8,128)(2,1)S(1)}, u32[]{:S(2)}, u32[]{:S(2)}) async-start(bf16[8,2,96,512]{3,2,1,0:T(8,128)(2,1)} %broadcast_in_dim.74), calls=%async_computation.1 | async-start | bytes 3145728 | tf_op jit(solution)/shard_map/all_to_all | solution.py:32
  41.7 78.1 %all-to-all-start.2 = ((bf16[8,192,2048]{2,1,0:T(8,128)(2,1)}), bf16[8,192,2048]{2,1,0:T(8,128)(2,1)}, u32[]{:S(2)}, u32[]{:S(2)}) async-start(bf16[8,192,2048]{2,1,0:T(8,128)(2,1)} %bitcast.40), calls=%async_computation.2 | async-start | bytes 12582912 | tf_op jit(solution)/shard_map/all_to_all | solution.py:55
  127.9 5.5 %copy-start.4 = (bf16[96,512]{1,0:T(8,128)(2,1)S(1)}, bf16[96,512]{1,0:T(8,128)(2,1)}, u32[]{:S(2)}) copy-start(bf16[96,512]{1,0:T(8,128)(2,1)} %param.8) | copy-start | bytes 294916
  127.9 111.4 %all-to-all-start.3 = ((bf16[8,192,2048]{2,1,0:T(8,128)(2,1)}), bf16[8,192,2048]{2,1,0:T(8,128)(2,1)}, u32[]{:S(2)}, u32[]{:S(2)}) async-start(bf16[8,192,2048]{2,1,0:T(8,128)(2,1)} %broadcast_in_dim.82), calls=%async_computation.3 | async-start | bytes 12582912 | tf_op jit(solution)/shard_map/all_to_all | solution.py:59
  134.2 71.6 %collective-permute-start.6 = (f32[13,1536]{1,0:T(8,128)S(1)}, f32[13,1536]{1,0:T(8,128)S(1)}, u32[]{:S(2)}, u32[]{:S(2)}) collective-permute-start(f32[13,1536]{1,0:T(8,128)S(1)} %get-tuple-element.18), channel_id=1, source_target_pairs={{0,7},{1,0},{2,1},{3,2},{4,3},{5,4},{6,5},{7,6},{8,15},{9,8},{10,9... | collective-permute-start | bytes 239624 | tf_op jit(solution)/shard_map/ppermute | solution.py:47
  139.8 68.8 %collective-permute-start.5 = (f32[13,1536]{1,0:T(8,128)S(1)}, f32[13,1536]{1,0:T(8,128)S(1)}, u32[]{:S(2)}, u32[]{:S(2)}) collective-permute-start(f32[13,1536]{1,0:T(8,128)S(1)} %get-tuple-element.13), channel_id=1, source_target_pairs={{0,6},{1,7},{2,0},{3,1},{4,2},{5,3},{6,4},{7,5},{8,14},{9,15},{10,... | collective-permute-start | bytes 239624 | tf_op jit(solution)/shard_map/ppermute | solution.py:47
  141.5 69.7 %collective-permute-start.4 = (f32[13,1536]{1,0:T(8,128)S(1)}, f32[13,1536]{1,0:T(8,128)S(1)}, u32[]{:S(2)}, u32[]{:S(2)}) collective-permute-start(f32[13,1536]{1,0:T(8,128)S(1)} %get-tuple-element.14), channel_id=1, source_target_pairs={{0,5},{1,6},{2,7},{3,0},{4,1},{5,2},{6,3},{7,4},{8,13},{9,14},{10,... | collective-permute-start | bytes 239624 | tf_op jit(solution)/shard_map/ppermute | solution.py:47
  142.4 70.3 %collective-permute-start.3 = (f32[13,1536]{1,0:T(8,128)S(1)}, f32[13,1536]{1,0:T(8,128)S(1)}, u32[]{:S(2)}, u32[]{:S(2)}) collective-permute-start(f32[13,1536]{1,0:T(8,128)S(1)} %get-tuple-element.15), channel_id=1, source_target_pairs={{0,4},{1,5},{2,6},{3,7},{4,0},{5,1},{6,2},{7,3},{8,12},{9,13},{10,... | collective-permute-start | bytes 239624 | tf_op jit(solution)/shard_map/ppermute | solution.py:47
  145.4 68.4 %collective-permute-start.2 = (f32[13,1536]{1,0:T(8,128)S(1)}, f32[13,1536]{1,0:T(8,128)S(1)}, u32[]{:S(2)}, u32[]{:S(2)}) collective-permute-start(f32[13,1536]{1,0:T(8,128)S(1)} %get-tuple-element.16), channel_id=1, source_target_pairs={{0,3},{1,4},{2,5},{3,6},{4,7},{5,0},{6,1},{7,2},{8,11},{9,12},{10,... | collective-permute-start | bytes 239624 | tf_op jit(solution)/shard_map/ppermute | solution.py:47
  205.8 9.9 %collective-permute-start.1 = (f32[13,1536]{1,0:T(8,128)S(1)}, f32[13,1536]{1,0:T(8,128)S(1)}, u32[]{:S(2)}, u32[]{:S(2)}) collective-permute-start(f32[13,1536]{1,0:T(8,128)S(1)} %get-tuple-element.17), channel_id=1, source_target_pairs={{0,2},{1,3},{2,4},{3,5},{4,6},{5,7},{6,0},{7,1},{8,10},{9,11},{10,... | collective-permute-start | bytes 239624 | tf_op jit(solution)/shard_map/ppermute | solution.py:47
  208.7 8.4 %collective-permute-start = (f32[13,1536]{1,0:T(8,128)S(1)}, f32[13,1536]{1,0:T(8,128)S(1)}, u32[]{:S(2)}, u32[]{:S(2)}) collective-permute-start(f32[13,1536]{1,0:T(8,128)S(1)} %get-tuple-element.12), channel_id=1, source_target_pairs={{0,1},{1,2},{2,3},{3,4},{4,5},{5,6},{6,7},{7,0},{8,9},{9,10},{10,1... | collective-permute-start | bytes 239624 | tf_op jit(solution)/shard_map/ppermute | solution.py:47
  217.8 13.2 %collective-permute-start.7 = (f32[13,1536]{1,0:T(8,128)}, f32[13,1536]{1,0:T(8,128)S(1)}, u32[]{:S(2)}, u32[]{:S(2)}) collective-permute-start(f32[13,1536]{1,0:T(8,128)} %get-tuple-element.9), channel_id=1, source_target_pairs={{0,1},{1,2},{2,3},{3,4},{4,5},{5,6},{6,7},{7,0},{8,9},{9,10},{10,1... | collective-permute-start | bytes 239624 | tf_op jit(solution)/shard_map/ppermute | solution.py:61
  219.0 16.5 %collective-permute-start.8 = (f32[13,1536]{1,0:T(8,128)}, f32[13,1536]{1,0:T(8,128)S(1)}, u32[]{:S(2)}, u32[]{:S(2)}) collective-permute-start(f32[13,1536]{1,0:T(8,128)} %get-tuple-element.9), channel_id=1, source_target_pairs={{0,2},{1,3},{2,4},{3,5},{4,6},{5,7},{6,0},{7,1},{8,10},{9,11},{10,... | collective-permute-start | bytes 239624 | tf_op jit(solution)/shard_map/ppermute | solution.py:61
  221.7 39.1 %collective-permute-start.9 = (f32[13,1536]{1,0:T(8,128)}, f32[13,1536]{1,0:T(8,128)}, u32[]{:S(2)}, u32[]{:S(2)}) collective-permute-start(f32[13,1536]{1,0:T(8,128)} %get-tuple-element.9), channel_id=1, source_target_pairs={{0,3},{1,4},{2,5},{3,6},{4,7},{5,0},{6,1},{7,2},{8,11},{9,12},{10,... | collective-permute-start | bytes 239624 | tf_op jit(solution)/shard_map/ppermute | solution.py:61
  227.2 35.1 %collective-permute-start.10 = (f32[13,1536]{1,0:T(8,128)}, f32[13,1536]{1,0:T(8,128)}, u32[]{:S(2)}, u32[]{:S(2)}) collective-permute-start(f32[13,1536]{1,0:T(8,128)} %get-tuple-element.9), channel_id=1, source_target_pairs={{0,4},{1,5},{2,6},{3,7},{4,0},{5,1},{6,2},{7,3},{8,12},{9,13},{10,... | collective-permute-start | bytes 239624 | tf_op jit(solution)/shard_map/ppermute | solution.py:61
  227.2 36.6 %collective-permute-start.11 = (f32[13,1536]{1,0:T(8,128)}, f32[13,1536]{1,0:T(8,128)S(1)}, u32[]{:S(2)}, u32[]{:S(2)}) collective-permute-start(f32[13,1536]{1,0:T(8,128)} %get-tuple-element.9), channel_id=1, source_target_pairs={{0,5},{1,6},{2,7},{3,0},{4,1},{5,2},{6,3},{7,4},{8,13},{9,14},{10,... | collective-permute-start | bytes 239624 | tf_op jit(solution)/shard_map/ppermute | solution.py:61
  231.0 33.5 %collective-permute-start.12 = (f32[13,1536]{1,0:T(8,128)}, f32[13,1536]{1,0:T(8,128)S(1)}, u32[]{:S(2)}, u32[]{:S(2)}) collective-permute-start(f32[13,1536]{1,0:T(8,128)} %get-tuple-element.9), channel_id=1, source_target_pairs={{0,6},{1,7},{2,0},{3,1},{4,2},{5,3},{6,4},{7,5},{8,14},{9,15},{10,... | collective-permute-start | bytes 239624 | tf_op jit(solution)/shard_map/ppermute | solution.py:61
  235.6 52.1 %collective-permute-start.13 = (f32[13,1536]{1,0:T(8,128)}, f32[13,1536]{1,0:T(8,128)}, u32[]{:S(2)}, u32[]{:S(2)}) collective-permute-start(f32[13,1536]{1,0:T(8,128)} %get-tuple-element.9), channel_id=1, source_target_pairs={{0,7},{1,0},{2,1},{3,2},{4,3},{5,4},{6,5},{7,6},{8,15},{9,8},{10,9... | collective-permute-start | bytes 239624 | tf_op jit(solution)/shard_map/ppermute | solution.py:61
  257.1 25.5 %all-to-all-start.5 = ((f32[8,96,512]{2,1,0:T(8,128)}), f32[8,96,512]{2,1,0:T(8,128)S(1)}, u32[]{:S(2)}, u32[]{:S(2)}) async-start(f32[8,96,512]{2,1,0:T(8,128)} %reduce_sum.47), calls=%async_computation.5 | async-start | bytes 3145728 | tf_op jit(solution)/shard_map/all_to_all | solution.py:75
  284.1 24.6 %all-to-all-start.6 = ((f32[8,96,512]{2,1,0:T(8,128)}), f32[8,96,512]{2,1,0:T(8,128)S(1)}, u32[]{:S(2)}, u32[]{:S(2)}) async-start(f32[8,96,512]{2,1,0:T(8,128)} %broadcast_in_dim.83), calls=%async_computation.6 | async-start | bytes 3145728 | tf_op jit(solution)/shard_map/all_to_all | solution.py:76
  295.1 0.8 copy-start.2
  315.8 1.1 copy-start.3
  315.8 3.9 %copy-start.1 = (f32[8192]{0:T(1024)S(1)}, f32[8192]{0:T(1024)}, u32[]{:S(2)}) copy-start(f32[8192]{0:T(1024)} %param.6) | copy-start | bytes 98308

commit v3 on v1

--- a/solution.py
+++ b/solution.py
@@ -26,11 +26,9 @@
     scale_h = spread[0].astype(jnp.float32)
     n_c = lax.axis_size("c")
     n_yx = lax.axis_size(YX)
-    pair_rows = lax.all_to_all(
-        jnp.broadcast_to(particles[None], (n_c,) + particles.shape), "c", 0, 0, tiled=True
-    )
+    n_dp = lax.axis_size(DP)
     all_rows = lax.all_to_all(
-        jnp.broadcast_to(pair_rows[None], (n_yx,) + pair_rows.shape), YX, 0, 0, tiled=True
+        jnp.broadcast_to(particles[None], (n_dp,) + particles.shape), DP, 0, 0, tiled=True
     ).reshape(-1, particles.shape[1])
     count_all = all_rows.shape[0]
     rows_own = particles.shape[0]

time: 342 us -> 339 us (level)
  blocking collectives: 95.6 us -> 91.7 us
    all_to_all x1 -> x0, blocking collectives: 3.89 us -> none  [step(): lax.all_to_all(jnp.broadcast_to(particles[None], (n_c,) + particles.shape...]
where the time goes in v3:
time: 339 us; the launch traced here: 337 us
  waiting for transfers between devices  149 us (44%)
  blocking collectives  91.7 us (27%)
  local copies, waits for them, and re-layouts  31.7 us (9%)
  starting transfers between devices  20.4 us (6%)
  matrix products  17.4 us (5%)
  between operations  14.9 us (4%)
  other arithmetic  12 us (4%)
    all_to_all x1, blocking collectives, step(): lax.all_to_all(spread_res, FT, 0, 0, tiled=True).reshape(count_all, -1)  78.2 us
    all_to_all x1, waiting for transfers between devices, step(): pieces = lax.all_to_all(partial_t, FT, 0, 0, tiled=True)  59.3 us
    psum x1, waiting for transfers between devices, step(): packed = lax.psum(to_sum, FT)  59.3 us
    all_to_all x1, waiting for transfers between devices, step(): grad_own = jnp.sum(lax.all_to_all(pair_sum, YX, 0, 0, tiled=True), axis=0)  21.9 us
    gather x1, local copies, waits for them, and re-layouts, step(): batch_x = jnp.take(dataset, indices, axis=0)  13.7 us
    gather x1, local copies, waits for them, and re-layouts, step(): batch_t = jnp.take(late[0], late[1], axis=0)  11.8 us
    all_to_all x1, waiting for transfers between devices, step(): lax.all_to_all(jnp.broadcast_to(particles[None], (n_dp,) + particles.shap...  8.46 us
    dot_general x2, matrix products, contract(): lax.dot_general(left, right, (((1,), (1,)), ((), ())), preferred_element_...  8.4 us
  transfers between devices with their start and end apart: 5, of which 4 were waited for; matrix products, arithmetic and copies ran while one was open for 10% of the time, Pallas kernels for 0%

profile of v3, /device:TPU:0, one launch (start us, length us, event | category | flops | bytes accessed | tf_op | source)
XLA Modules:
  0.0 337.1 jit_solution(697221844282309869)
XLA Ops:
  7.2 0.0 copy-start
  7.2 0.0 copy-start.5
  7.2 2.2 broadcast_in_dim.50
  9.4 5.6 %all-to-all-start = ((bf16[16,96,512]{2,1,0:T(8,128)(2,1)}), bf16[16,96,512]{2,1,0:T(8,128)(2,1)S(1)}, u32[]{:S(2)}, u32[]{:S(2)}) async-start(bf16[16,96,512]{2,1,0:T(8,128)(2,1)} %broadcast_in_dim.50), calls=%async_computation | async-start | bytes 3145728 | tf_op jit(solution)/shard_map/all_to_all | solution.py:30
  15.0 0.0 copy-done.5
  15.0 13.7 %gather_fusion = bf16[2048,512]{1,0:T(8,128)(2,1)} fusion(bf16[8192,512]{1,0:T(8,128)(2,1)} %param.5, s32[2048]{0:T(1024)S(1)} %fusion.8), kind=kCustom, calls=%fused_computation | custom fusion | bytes 4202496 | tf_op jit(solution)/shard_map/jit(_take)/gather | solution.py:24
  28.8 8.5 %all-to-all-done = bf16[16,96,512]{2,1,0:T(8,128)(2,1)S(1)} async-done(((bf16[16,96,512]{2,1,0:T(8,128)(2,1)}), bf16[16,96,512]{2,1,0:T(8,128)(2,1)S(1)}, u32[]{:S(2)}, u32[]{:S(2)}) %all-to-all-start) | async-done | bytes 1572896 | tf_op jit(solution)/shard_map/all_to_all | solution.py:30
  37.2 7.8 %convolution_convert_fusion = bf16[2048,1536]{0,1:T(8,128)(2,1)} fusion(bf16[1536,512]{1,0:T(8,128)(2,1)S(1)} %bitcast.19, bf16[2048,512]{1,0:T(8,128)(2,1)} %gather_fusion, pred[2048]{0:T(1024)(128)(4,1)S(1)} %compare_and_fusion), kind=kOutput, calls=%fused_computation.3 | convolution fusion | flops 3225419776 | bytes 9963520 | tf_op jit(solution)/shard_map/dot_general | solution.py:13
  45.0 7.5 %all-to-all-start.1 = ((bf16[8,192,2048]{2,1,0:T(8,128)(2,1)}), bf16[8,192,2048]{2,1,0:T(8,128)(2,1)}, u32[]{:S(2)}, u32[]{:S(2)}) async-start(bf16[8,192,2048]{2,1,0:T(8,128)(2,1)} %bitcast.22), calls=%async_computation.1 | async-start | bytes 12582912 | tf_op jit(solution)/shard_map/all_to_all | solution.py:44
  52.5 0.0 copy-done
  52.5 11.8 %gather_fusion.1 = f32[2048]{0:T(1024)S(1)} fusion(f32[8192]{0:T(1024)S(1)} %copy-done, s32[2048]{0:T(1024)S(1)} %fusion.9), kind=kCustom, calls=%fused_computation.1 | custom fusion | bytes 24576 | tf_op jit(solution)/shard_map/jit(_take)/gather | solution.py:43
  64.3 59.3 %all-to-all-done.1 = bf16[8,192,2048]{2,1,0:T(8,128)(2,1)} async-done(((bf16[8,192,2048]{2,1,0:T(8,128)(2,1)}), bf16[8,192,2048]{2,1,0:T(8,128)(2,1)}, u32[]{:S(2)}, u32[]{:S(2)}) %all-to-all-start.1) | async-done | bytes 6291488 | tf_op jit(solution)/shard_map/all_to_all | solution.py:44
  123.7 4.2 %convert_reduce_fusion = f32[192,2048]{1,0:T(8,128)S(1)} fusion(bf16[8,192,2048]{2,1,0:T(8,128)(2,1)} %all-to-all-done.1), kind=kLoop, calls=%fused_computation.2 | loop fusion | flops 5898240 | bytes 7864320 | tf_op jit(solution)/shard_map/reduce_sum | solution.py:45
  127.8 0.4 subtract_convert_fusion
  128.3 0.8 broadcast_in_dim.57
  129.0 0.0 copy-start.3
  129.1 78.2 %all_to_all.35 = bf16[8,192,2048]{2,1,0:T(8,128)(2,1)S(1)} all-to-all(bf16[8,192,2048]{2,1,0:T(8,128)(2,1)S(1)} %broadcast_in_dim.57), channel_id=1, replica_groups=mesh['y'=4,'xl'=2,'c'=2,'xh'=2,'z'=4] {'xh','z'}, dimensions={0} | all-to-all | bytes 12582912 | tf_op jit(solution)/shard_map/all_to_all | solution.py:48
  207.3 0.0 copy-done.3
  207.3 3.5 %fusion = f32[8,2,96,512]{3,2,0,1:T(8,128)S(1)} fusion(bf16[8,2,96,2048]{3,2,1,0:T(8,128)(2,1)S(1)} %bitcast.23, bf16[2048,512]{1,0:T(8,128)(2,1)S(1)} %copy-done.3, pred[2048]{0:T(1024)(128)(4,1)S(1)} %compare_and_fusion), kind=kOutput, calls=%fused_computation.4 | convolution fusion | flops 3222274048 | bytes 11536384 | tf_op jit(solution)/shard_map/dot_general | solution.py:53
  210.8 7.2 %all_to_all.36 = f32[8,2,96,512]{3,2,0,1:T(8,128)} all-to-all(f32[8,2,96,512]{3,2,0,1:T(8,128)S(1)} %fusion), channel_id=1, replica_groups=mesh['y'=4,'xl'=2,'c'=2,'xh'=2,'z'=4] {'c'}, dimensions={1} | all-to-all | bytes 6291456 | tf_op jit(solution)/shard_map/all_to_all | solution.py:55
  218.0 3.5 %reduce_sum.47 = f32[8,96,512]{2,1,0:T(8,128)} reduce(f32[8,2,96,512]{3,2,0,1:T(8,128)} %all_to_all.36, f32[]{:T(128)} %constant.27.clone.1), dimensions={1}, to_apply=%region_3.4 | reduce | flops 393216 | bytes 4718596 | tf_op jit(solution)/shard_map/reduce_sum | solution.py:58
  221.5 3.7 %all-to-all-start.4 = ((f32[8,96,512]{2,1,0:T(8,128)}), f32[8,96,512]{2,1,0:T(8,128)S(1)}, u32[]{:S(2)}, u32[]{:S(2)}) async-start(f32[8,96,512]{2,1,0:T(8,128)} %reduce_sum.47), calls=%async_computation.4 | async-start | bytes 3145728 | tf_op jit(solution)/shard_map/all_to_all | solution.py:59
  225.3 0.0 all-reduce.2.cloned.1.call-start
  225.3 0.4 multiply_reduce_fusion
  225.7 0.1 broadcast_in_dim.51
  225.8 0.0 copy-done.4
  225.8 0.6 fusion.16
  226.4 0.9 pad_maximum_fusion
  227.3 0.0 all-reduce.2.cloned.1.call-update
  227.3 21.9 %all-to-all-done.4 = f32[8,96,512]{2,1,0:T(8,128)S(1)} async-done(((f32[8,96,512]{2,1,0:T(8,128)}), f32[8,96,512]{2,1,0:T(8,128)S(1)}, u32[]{:S(2)}, u32[]{:S(2)}) %all-to-all-start.4) | async-done | bytes 1572896 | tf_op jit(solution)/shard_map/all_to_all | solution.py:59
  249.3 0.1 reduce_sum.48
  249.4 1.4 broadcast_in_dim.58
  250.8 3.6 %all-to-all-start.5 = ((f32[8,96,512]{2,1,0:T(8,128)}), f32[8,96,512]{2,1,0:T(8,128)S(1)}, u32[]{:S(2)}, u32[]{:S(2)}) async-start(f32[8,96,512]{2,1,0:T(8,128)} %broadcast_in_dim.58), calls=%async_computation.5 | async-start | bytes 3145728 | tf_op jit(solution)/shard_map/all_to_all | solution.py:60
  255.0 59.3 %all-reduce.2.cloned.1.call-done = f32[97,1536]{1,0:T(8,128)} async-done(((f32[97,1536]{1,0:T(8,128)}), f32[97,1536]{1,0:T(8,128)}) %all-reduce.2.cloned.1.call-update) | async-done | bytes 595984 | tf_op jit(solution)/shard_map/psum | solution.py:49
  314.3 0.8 fusion.15
  315.1 0.1 dynamic-slice_bitcast_fusion
  315.2 1.4 fusion.13
  316.6 2.7 fusion.3
  319.3 0.0 all-to-all-done.5
  319.3 0.4 broadcast_in_dim.59
  319.7 6.3 %all_to_all.37 = f32[8,2,96,512]{3,2,0,1:T(8,128)S(1)} all-to-all(f32[8,2,96,512]{3,2,0,1:T(8,128)S(1)} %broadcast_in_dim.59), channel_id=1, replica_groups=mesh['y'=4,'xl'=2,'c'=2,'xh'=2,'z'=4] {'c'}, dimensions={1} | all-to-all | bytes 6291456 | tf_op jit(solution)/shard_map/all_to_all | solution.py:63
  326.0 0.4 copy_multiply_fusion
  326.4 0.0 copy-start.2
  326.4 0.0 copy-start.1
  326.4 0.6 bitcast_subtract_fusion
  327.0 0.4 copy-done.2
  327.5 2.8 convolution_multiply_fusion
  330.3 0.0 copy-done.1
  (5 shorter events, 0.0 us)
Async XLA Ops:
  7.2 45.3 %copy-start = (f32[8192]{0:T(1024)S(1)}, f32[8192]{0:T(1024)}, u32[]{:S(2)}) copy-start(f32[8192]{0:T(1024)} %param.6) | copy-start | bytes 98308
  7.2 7.8 %copy-start.5 = (s32[2048]{0:T(1024)S(1)}, s32[2048]{0:T(1024)}, u32[]{:S(2)}) copy-start(s32[2048]{0:T(1024)} %param.7) | copy-start | bytes 24580
  9.4 27.8 %all-to-all-start = ((bf16[16,96,512]{2,1,0:T(8,128)(2,1)}), bf16[16,96,512]{2,1,0:T(8,128)(2,1)S(1)}, u32[]{:S(2)}, u32[]{:S(2)}) async-start(bf16[16,96,512]{2,1,0:T(8,128)(2,1)} %broadcast_in_dim.50), calls=%async_computation | async-start | bytes 3145728 | tf_op jit(solution)/shard_map/all_to_all | solution.py:30
  45.0 78.6 %all-to-all-start.1 = ((bf16[8,192,2048]{2,1,0:T(8,128)(2,1)}), bf16[8,192,2048]{2,1,0:T(8,128)(2,1)}, u32[]{:S(2)}, u32[]{:S(2)}) async-start(bf16[8,192,2048]{2,1,0:T(8,128)(2,1)} %bitcast.22), calls=%async_computation.1 | async-start | bytes 12582912 | tf_op jit(solution)/shard_map/all_to_all | solution.py:44
  129.0 78.2 %copy-start.3 = (bf16[2048,512]{1,0:T(8,128)(2,1)S(1)}, bf16[2048,512]{1,0:T(8,128)(2,1)}, u32[]{:S(2)}) copy-start(bf16[2048,512]{1,0:T(8,128)(2,1)} %gather_fusion) | copy-start | bytes 6291460
  221.5 4.3 %copy-start.4 = (bf16[96,512]{1,0:T(8,128)(2,1)S(1)}, bf16[96,512]{1,0:T(8,128)(2,1)}, u32[]{:S(2)}) copy-start(bf16[96,512]{1,0:T(8,128)(2,1)} %param.8) | copy-start | bytes 294916
  221.5 27.7 %all-to-all-start.4 = ((f32[8,96,512]{2,1,0:T(8,128)}), f32[8,96,512]{2,1,0:T(8,128)S(1)}, u32[]{:S(2)}, u32[]{:S(2)}) async-start(f32[8,96,512]{2,1,0:T(8,128)} %reduce_sum.47), calls=%async_computation.4 | async-start | bytes 3145728 | tf_op jit(solution)/shard_map/all_to_all | solution.py:59
  225.3 89.0 %all-reduce.2.cloned.1.call-start = ((), (), s32[]{:S(2)}) async-start(), calls=%async_computation.7 | async-start | bytes 1277952 | tf_op jit(solution)/shard_map/psum | solution.py:49
  250.8 68.5 %all-to-all-start.5 = ((f32[8,96,512]{2,1,0:T(8,128)}), f32[8,96,512]{2,1,0:T(8,128)S(1)}, u32[]{:S(2)}, u32[]{:S(2)}) async-start(f32[8,96,512]{2,1,0:T(8,128)} %broadcast_in_dim.58), calls=%async_computation.5 | async-start | bytes 3145728 | tf_op jit(solution)/shard_map/all_to_all | solution.py:60
  326.4 1.1 copy-start.2
  326.4 3.9 %copy-start.1 = (f32[8192]{0:T(1024)S(1)}, f32[8192]{0:T(1024)}, u32[]{:S(2)}) copy-start(f32[8192]{0:T(1024)} %param.6) | copy-start | bytes 98308
Sparse Core Ops, SparseCore 0:
  228.6 85.6 all-reduce.1

commit v4 on v3

--- a/solution.py
+++ b/solution.py
@@ -60,12 +60,24 @@
     chips = lax.all_to_all(
         jnp.broadcast_to(grad_own[None], (n_yx,) + grad_own.shape), YX, 0, 0, tiled=True
     )
-    gradient = lax.all_to_all(
+    kernel = jnp.exp(-(own_sq[:, None] + norms_b[None, :] - 2.0 * inner) / scale_h)
+    kernel4 = kernel.reshape(rows_own, n_yx, n_c, rows_own)
+    theta4 = theta_all.reshape(n_yx, n_c, rows_own, width)
+    me_c = lax.axis_index("c")
+    mine = lambda a, axis: lax.dynamic_index_in_dim(a, me_c, axis, keepdims=False)
+    score_own = data_ratio * chips - mine(theta4, 1)
+    pushed = lax.optimization_barrier(exact_dot(
+        mine(kernel4, 2).reshape(rows_own, -1), score_own.reshape(-1, width)
+    ))
+    both = lax.all_to_all(
         jnp.broadcast_to(chips[:, None], (n_yx, n_c, rows_own, width)), "c", 1, 1, tiled=True
-    ).reshape(count_all, width)
-    score = data_ratio * gradient - theta_all
-    kernel = jnp.exp(-(own_sq[:, None] + norms_b[None, :] - 2.0 * inner) / scale_h)
-    pushed = exact_dot(kernel, score)
+    )
+    other = 1 - me_c
+    theirs = lambda a, axis: lax.dynamic_index_in_dim(a, other, axis, keepdims=False)
+    score_other = data_ratio * theirs(both, 1) - theirs(theta4, 1)
+    pushed = pushed + exact_dot(
+        theirs(kernel4, 2).reshape(rows_own, -1), score_other.reshape(-1, width)
+    )
     pulled = exact_dot(kernel, theta_all)
     weight = jnp.sum(kernel, axis=1)
     attraction = pushed / count_all

time: 339 us -> 349 us (1.029)
  local copies, waits for them, and re-layouts: 31.7 us -> 39.1 us
  other arithmetic: 12 us -> 15.7 us
    reshape x0 -> x2, local copies, waits for them, and re-layouts: none -> 4.16 us  [the longest x1 3.01 us: step(): kernel4 = kernel.reshape(rows_own, n_yx, n_c, rows_own)]
    dynamic_slice x0 -> x1, local copies, waits for them, and re-layouts: none -> 3.69 us  [step(): lax.dynamic_index_in_dim(a, other, axis, keepdims=False)]
  transfers between devices with their start and end apart: 5 -> 5, of which waited for: 4 -> 4; matrix products, arithmetic and copies ran while one was open for 10% -> 13% of each run, Pallas kernels for 0% -> 0%
where the time goes in v4:
time: 349 us; the launch traced here: 347 us
  waiting for transfers between devices  147 us (42%)
  blocking collectives  91.9 us (26%)
  local copies, waits for them, and re-layouts  39.1 us (11%)
  starting transfers between devices  20.4 us (6%)
  matrix products  17.6 us (5%)
  other arithmetic  15.7 us (4%)
  between operations  14.9 us (4%)
    all_to_all x1, blocking collectives, step(): lax.all_to_all(spread_res, FT, 0, 0, tiled=True).reshape(count_all, -1)  78.2 us
    all_to_all x1, waiting for transfers between devices, step(): pieces = lax.all_to_all(partial_t, FT, 0, 0, tiled=True)  59.3 us
    psum x1, waiting for transfers between devices, step(): packed = lax.psum(to_sum, FT)  57.2 us
    all_to_all x1, waiting for transfers between devices, step(): grad_own = jnp.sum(lax.all_to_all(pair_sum, YX, 0, 0, tiled=True), axis=0)  21.9 us
    gather x1, local copies, waits for them, and re-layouts, step(): batch_x = jnp.take(dataset, indices, axis=0)  13.7 us
    gather x1, local copies, waits for them, and re-layouts, step(): batch_t = jnp.take(late[0], late[1], axis=0)  11.8 us
    all_to_all x1, waiting for transfers between devices, step(): lax.all_to_all(jnp.broadcast_to(particles[None], (n_dp,) + particles.shap...  8.46 us
    dot_general x2, matrix products, contract(): lax.dot_general(left, right, (((1,), (1,)), ((), ())), preferred_element_...  8.4 us
  transfers between devices with their start and end apart: 5, of which 4 were waited for; matrix products, arithmetic and copies ran while one was open for 13% of the time, Pallas kernels for 0%

profile of v4, /device:TPU:0, one launch (start us, length us, event | category | flops | bytes accessed | tf_op | source)
XLA Modules:
  0.0 346.6 jit_solution(3392161626521238126)
XLA Ops:
  7.2 0.0 copy-start
  7.2 0.0 copy-start.6
  7.2 2.2 broadcast_in_dim.50
  9.4 5.6 %all-to-all-start = ((bf16[16,96,512]{2,1,0:T(8,128)(2,1)}), bf16[16,96,512]{2,1,0:T(8,128)(2,1)S(1)}, u32[]{:S(2)}, u32[]{:S(2)}) async-start(bf16[16,96,512]{2,1,0:T(8,128)(2,1)} %broadcast_in_dim.50), calls=%async_computation | async-start | bytes 3145728 | tf_op jit(solution)/shard_map/all_to_all | solution.py:30
  15.0 0.0 copy-done.6
  15.0 13.7 %gather_fusion = bf16[2048,512]{1,0:T(8,128)(2,1)} fusion(bf16[8192,512]{1,0:T(8,128)(2,1)} %param.5, s32[2048]{0:T(1024)S(1)} %fusion.26), kind=kCustom, calls=%fused_computation | custom fusion | bytes 4202496 | tf_op jit(solution)/shard_map/jit(_take)/gather | solution.py:24
  28.8 8.5 %all-to-all-done = bf16[16,96,512]{2,1,0:T(8,128)(2,1)S(1)} async-done(((bf16[16,96,512]{2,1,0:T(8,128)(2,1)}), bf16[16,96,512]{2,1,0:T(8,128)(2,1)S(1)}, u32[]{:S(2)}, u32[]{:S(2)}) %all-to-all-start) | async-done | bytes 1572896 | tf_op jit(solution)/shard_map/all_to_all | solution.py:30
  37.2 7.8 %convolution_convert_fusion = bf16[2048,1536]{0,1:T(8,128)(2,1)} fusion(bf16[1536,512]{1,0:T(8,128)(2,1)S(1)} %bitcast.54, bf16[2048,512]{1,0:T(8,128)(2,1)} %gather_fusion, pred[2048]{0:T(1024)(128)(4,1)S(1)} %compare_and_fusion), kind=kOutput, calls=%fused_computation.3 | convolution fusion | flops 3225419776 | bytes 9963520 | tf_op jit(solution)/shard_map/dot_general | solution.py:13
  45.0 7.5 %all-to-all-start.1 = ((bf16[8,192,2048]{2,1,0:T(8,128)(2,1)}), bf16[8,192,2048]{2,1,0:T(8,128)(2,1)}, u32[]{:S(2)}, u32[]{:S(2)}) async-start(bf16[8,192,2048]{2,1,0:T(8,128)(2,1)} %bitcast.58), calls=%async_computation.1 | async-start | bytes 12582912 | tf_op jit(solution)/shard_map/all_to_all | solution.py:44
  52.5 0.0 copy-done
  52.5 11.8 %gather_fusion.1 = f32[2048]{0:T(1024)S(1)} fusion(f32[8192]{0:T(1024)S(1)} %copy-done, s32[2048]{0:T(1024)S(1)} %fusion.27), kind=kCustom, calls=%fused_computation.1 | custom fusion | bytes 24576 | tf_op jit(solution)/shard_map/jit(_take)/gather | solution.py:43
  64.3 59.3 %all-to-all-done.1 = bf16[8,192,2048]{2,1,0:T(8,128)(2,1)} async-done(((bf16[8,192,2048]{2,1,0:T(8,128)(2,1)}), bf16[8,192,2048]{2,1,0:T(8,128)(2,1)}, u32[]{:S(2)}, u32[]{:S(2)}) %all-to-all-start.1) | async-done | bytes 6291488 | tf_op jit(solution)/shard_map/all_to_all | solution.py:44
  123.7 4.2 %convert_reduce_fusion = f32[192,2048]{1,0:T(8,128)S(1)} fusion(bf16[8,192,2048]{2,1,0:T(8,128)(2,1)} %all-to-all-done.1), kind=kLoop, calls=%fused_computation.2 | loop fusion | flops 5898240 | bytes 7864320 | tf_op jit(solution)/shard_map/reduce_sum | solution.py:45
  127.8 0.4 subtract_convert_fusion
  128.3 0.8 broadcast_in_dim.57
  129.1 78.2 %all_to_all.35 = bf16[8,192,2048]{2,1,0:T(8,128)(2,1)S(1)} all-to-all(bf16[8,192,2048]{2,1,0:T(8,128)(2,1)S(1)} %broadcast_in_dim.57), channel_id=1, replica_groups=mesh['y'=4,'xl'=2,'c'=2,'xh'=2,'z'=4] {'xh','z'}, dimensions={0} | all-to-all | bytes 12582912 | tf_op jit(solution)/shard_map/all_to_all | solution.py:48
  207.3 3.5 %fusion = f32[8,2,96,512]{3,2,0,1:T(8,128)S(1)} fusion(bf16[8,2,96,2048]{3,2,1,0:T(8,128)(2,1)S(1)} %bitcast.59, bf16[2048,512]{1,0:T(8,128)(2,1)S(1)} %copy-done.3, pred[2048]{0:T(1024)(128)(4,1)S(1)} %compare_and_fusion), kind=kOutput, calls=%fused_computation.4 | convolution fusion | flops 3222274048 | bytes 11536384 | tf_op jit(solution)/shard_map/dot_general | solution.py:53
  210.8 7.2 %all_to_all.36 = f32[8,2,96,512]{3,2,0,1:T(8,128)} all-to-all(f32[8,2,96,512]{3,2,0,1:T(8,128)S(1)} %fusion), channel_id=1, replica_groups=mesh['y'=4,'xl'=2,'c'=2,'xh'=2,'z'=4] {'c'}, dimensions={1} | all-to-all | bytes 6291456 | tf_op jit(solution)/shard_map/all_to_all | solution.py:55
  218.0 3.5 %reduce_sum.47 = f32[8,96,512]{2,1,0:T(8,128)} reduce(f32[8,2,96,512]{3,2,0,1:T(8,128)} %all_to_all.36, f32[]{:T(128)} %constant.64.clone.1), dimensions={1}, to_apply=%region_3.4 | reduce | flops 393216 | bytes 4718596 | tf_op jit(solution)/shard_map/reduce_sum | solution.py:58
  221.5 3.7 %all-to-all-start.4 = ((f32[8,96,512]{2,1,0:T(8,128)}), f32[8,96,512]{2,1,0:T(8,128)S(1)}, u32[]{:S(2)}, u32[]{:S(2)}) async-start(f32[8,96,512]{2,1,0:T(8,128)} %reduce_sum.47), calls=%async_computation.4 | async-start | bytes 3145728 | tf_op jit(solution)/shard_map/all_to_all | solution.py:59
  225.3 0.0 all-reduce.2.cloned.1.call-start
  225.3 0.4 multiply_reduce_fusion
  225.7 0.1 broadcast_in_dim.51
  225.8 0.0 copy-done.5
  225.8 0.6 fusion.36
  226.4 0.9 pad_maximum_fusion
  227.3 0.0 all-reduce.2.cloned.1.call-update
  227.4 21.9 %all-to-all-done.4 = f32[8,96,512]{2,1,0:T(8,128)S(1)} async-done(((f32[8,96,512]{2,1,0:T(8,128)}), f32[8,96,512]{2,1,0:T(8,128)S(1)}, u32[]{:S(2)}, u32[]{:S(2)}) %all-to-all-start.4) | async-done | bytes 1572896 | tf_op jit(solution)/shard_map/all_to_all | solution.py:59
  249.3 0.1 reduce_sum.48
  249.4 1.3 broadcast_in_dim.58
  250.8 3.6 %all-to-all-start.5 = ((f32[8,96,512]{2,1,0:T(8,128)}), f32[8,96,512]{2,1,0:T(8,128)S(1)}, u32[]{:S(2)}, u32[]{:S(2)}) async-start(f32[8,96,512]{2,1,0:T(8,128)} %broadcast_in_dim.58), calls=%async_computation.5 | async-start | bytes 3145728 | tf_op jit(solution)/shard_map/all_to_all | solution.py:60
  255.0 2.1 convert.3
  257.1 57.2 %all-reduce.2.cloned.1.call-done = f32[97,1536]{1,0:T(8,128)} async-done(((f32[97,1536]{1,0:T(8,128)}), f32[97,1536]{1,0:T(8,128)}) %all-reduce.2.cloned.1.call-update) | async-done | bytes 595984 | tf_op jit(solution)/shard_map/psum | solution.py:49
  314.3 0.8 fusion.35
  315.1 0.1 fusion.29
  315.2 2.2 fusion.33
  317.4 3.0 reshape.88
  320.5 3.7 %constant_dynamic-slice_fusion = (f32[96,8,1,96]{3,2,1,0:T(1,128)}, f32[96,8,96]{2,1,0:T(8,128)}) fusion(f32[96,8,2,96]{3,2,1,0:T(2,128)} %reshape.88, s32[]{:T(128)S(6)} %select_n.39, s32[]{:T(128)S(6)} %select_n.34), kind=kLoop, calls=%fused_computation.39 | loop fusion | bytes 1179656 | tf_op jit(solution)/shard_map/jit(dynamic_index_in_dim)/dynamic_slice | solution.py:76
  324.2 1.1 reshape.89
  325.3 2.6 fusion.12
  327.9 0.0 all-to-all-done.5
  327.9 1.8 bitcast_subtract_fusion
  329.7 1.0 fusion.37
  330.8 0.4 broadcast_in_dim.59
  331.2 0.0 copy-start.1
  331.2 6.5 %all_to_all.37 = f32[8,2,96,512]{3,2,0,1:T(8,128)S(1)} all-to-all(f32[8,2,96,512]{3,2,0,1:T(8,128)S(1)} %broadcast_in_dim.59), channel_id=1, replica_groups=mesh['y'=4,'xl'=2,'c'=2,'xh'=2,'z'=4] {'c'}, dimensions={1} | all-to-all | bytes 6291456 | tf_op jit(solution)/shard_map/all_to_all | solution.py:72
  337.7 2.0 fusion.16
  339.8 0.0 copy-done.1
  (11 shorter events, 0.0 us)
Async XLA Ops:
  7.2 45.3 %copy-start = (f32[8192]{0:T(1024)S(1)}, f32[8192]{0:T(1024)}, u32[]{:S(2)}) copy-start(f32[8192]{0:T(1024)} %param.6) | copy-start | bytes 98308
  7.2 7.8 %copy-start.6 = (s32[2048]{0:T(1024)S(1)}, s32[2048]{0:T(1024)}, u32[]{:S(2)}) copy-start(s32[2048]{0:T(1024)} %param.7) | copy-start | bytes 24580
  9.4 27.8 %all-to-all-start = ((bf16[16,96,512]{2,1,0:T(8,128)(2,1)}), bf16[16,96,512]{2,1,0:T(8,128)(2,1)S(1)}, u32[]{:S(2)}, u32[]{:S(2)}) async-start(bf16[16,96,512]{2,1,0:T(8,128)(2,1)} %broadcast_in_dim.50), calls=%async_computation | async-start | bytes 3145728 | tf_op jit(solution)/shard_map/all_to_all | solution.py:30
  45.0 78.6 %all-to-all-start.1 = ((bf16[8,192,2048]{2,1,0:T(8,128)(2,1)}), bf16[8,192,2048]{2,1,0:T(8,128)(2,1)}, u32[]{:S(2)}, u32[]{:S(2)}) async-start(bf16[8,192,2048]{2,1,0:T(8,128)(2,1)} %bitcast.58), calls=%async_computation.1 | async-start | bytes 12582912 | tf_op jit(solution)/shard_map/all_to_all | solution.py:44
  129.0 78.2 %copy-start.3 = (bf16[2048,512]{1,0:T(8,128)(2,1)S(1)}, bf16[2048,512]{1,0:T(8,128)(2,1)}, u32[]{:S(2)}) copy-start(bf16[2048,512]{1,0:T(8,128)(2,1)} %gather_fusion) | copy-start | bytes 6291460
  221.5 4.3 %copy-start.5 = (bf16[96,512]{1,0:T(8,128)(2,1)S(1)}, bf16[96,512]{1,0:T(8,128)(2,1)}, u32[]{:S(2)}) copy-start(bf16[96,512]{1,0:T(8,128)(2,1)} %param.8) | copy-start | bytes 294916
  221.5 27.7 %all-to-all-start.4 = ((f32[8,96,512]{2,1,0:T(8,128)}), f32[8,96,512]{2,1,0:T(8,128)S(1)}, u32[]{:S(2)}, u32[]{:S(2)}) async-start(f32[8,96,512]{2,1,0:T(8,128)} %reduce_sum.47), calls=%async_computation.4 | async-start | bytes 3145728 | tf_op jit(solution)/shard_map/all_to_all | solution.py:59
  225.3 89.0 %all-reduce.2.cloned.1.call-start = ((), (), s32[]{:S(2)}) async-start(), calls=%async_computation.7 | async-start | bytes 1277952 | tf_op jit(solution)/shard_map/psum | solution.py:49
  250.8 77.2 %all-to-all-start.5 = ((f32[8,96,512]{2,1,0:T(8,128)}), f32[8,96,512]{2,1,0:T(8,128)S(1)}, u32[]{:S(2)}, u32[]{:S(2)}) async-start(f32[8,96,512]{2,1,0:T(8,128)} %broadcast_in_dim.58), calls=%async_computation.5 | async-start | bytes 3145728 | tf_op jit(solution)/shard_map/all_to_all | solution.py:60
  331.2 6.6 %copy-start.2 = (f32[8,2,96,512]{3,2,1,0:T(8,128)S(1)}, f32[8,2,96,512]{3,2,1,0:T(8,128)}, u32[]{:S(2)}) copy-start(f32[8,2,96,512]{3,2,1,0:T(8,128)} %convert.3) | copy-start | bytes 9437188
  331.2 6.6 %copy-start.4 = (f32[96,8,1,96]{3,2,1,0:T(1,128)S(1)}, f32[96,8,1,96]{3,2,1,0:T(1,128)}, u32[]{:S(2)}) copy-start(f32[96,8,1,96]{3,2,1,0:T(1,128)} %get-tuple-element.10) | copy-start | bytes 884740
  331.2 8.6 %copy-start.1 = (f32[8192]{0:T(1024)S(1)}, f32[8192]{0:T(1024)}, u32[]{:S(2)}) copy-start(f32[8192]{0:T(1024)} %param.6) | copy-start | bytes 98308
Sparse Core Ops, SparseCore 0:
  228.6 85.6 all-reduce.1

commit v5 on v3

--- a/solution.py
+++ b/solution.py
@@ -52,24 +52,29 @@
     own_sq = lax.dynamic_slice_in_dim(norms_b, lax.axis_index(DP) * rows_own, rows_own, 0)
     grad_part = jnp.dot(residual_t, batch_x, preferred_element_type=jnp.float32)
     width = grad_part.shape[1]
-    pair = lax.all_to_all(
-        grad_part.reshape(n_yx, n_c, rows_own, width), "c", 1, 1, tiled=True
+    me_c = lax.axis_index("c")
+    swap = [(0, 1), (1, 0)]
+    grad4 = grad_part.reshape(n_yx, n_c, rows_own, width)
+    from_pair = lax.ppermute(
+        lax.dynamic_index_in_dim(grad4, 1 - me_c, 1, keepdims=False), "c", swap
     )
-    pair_sum = jnp.sum(pair, axis=1)
+    pair_sum = lax.dynamic_index_in_dim(grad4, me_c, 1, keepdims=False) + from_pair
     grad_own = jnp.sum(lax.all_to_all(pair_sum, YX, 0, 0, tiled=True), axis=0)
     chips = lax.all_to_all(
         jnp.broadcast_to(grad_own[None], (n_yx,) + grad_own.shape), YX, 0, 0, tiled=True
     )
-    gradient = lax.all_to_all(
-        jnp.broadcast_to(chips[:, None], (n_yx, n_c, rows_own, width)), "c", 1, 1, tiled=True
+    other_chips = lax.ppermute(chips, "c", swap)
+    first = me_c == 0
+    gradient = jnp.stack(
+        [jnp.where(first, chips, other_chips), jnp.where(first, other_chips, chips)], axis=1
     ).reshape(count_all, width)
     score = data_ratio * gradient - theta_all
     kernel = jnp.exp(-(own_sq[:, None] + norms_b[None, :] - 2.0 * inner) / scale_h)
-    pushed = exact_dot(kernel, score)
     pulled = exact_dot(kernel, theta_all)
     weight = jnp.sum(kernel, axis=1)
+    repulsion = (particles.astype(jnp.float32) * weight[:, None] - pulled) / count_all
+    pushed = exact_dot(kernel, score)
     attraction = pushed / count_all
-    repulsion = (particles.astype(jnp.float32) * weight[:, None] - pulled) / count_all
     return attraction, repulsion
 
 

time: 339 us -> 379 us (1.12)
  waiting for transfers between devices: 149 us -> 245 us
  blocking collectives: 91.7 us -> 24.3 us
  local copies, waits for them, and re-layouts: 31.7 us -> 36.9 us
  matrix products: 17.4 us -> 21.6 us
    all_to_all x3 -> x1, blocking collectives: 91.7 us -> 24.3 us  [step(): grad_own = jnp.sum(lax.all_to_all(pair_sum, YX, 0, 0, tiled=True), axis=0)]
    all_to_all x1, waiting for transfers between devices: 21.9 us -> 71.6 us  [step(): lax.all_to_all(spread_res, FT, 0, 0, tiled=True).reshape(count_all, -1)]
    psum x1, waiting for transfers between devices: 59.3 us -> 83.1 us  [step(): packed = lax.psum(to_sum, FT)]
    all_to_all x1, waiting for transfers between devices: 0.01 us -> 19 us  [step(): lax.all_to_all(jnp.broadcast_to(grad_own[None], (n_yx,) + grad_own.shape)...]
  transfers between devices with their start and end apart: 5 -> 7, of which waited for: 4 -> 6; matrix products, arithmetic and copies ran while one was open for 10% -> 9% of each run, Pallas kernels for 0% -> 0%
where the time goes in v5:
time: 379 us; the launch traced here: 378 us
  waiting for transfers between devices  245 us (65%)
  local copies, waits for them, and re-layouts  36.9 us (10%)
  blocking collectives  24.3 us (6%)
  starting transfers between devices  21.6 us (6%)
  matrix products  21.6 us (6%)
  between operations  14.9 us (4%)
  other arithmetic  13.1 us (3%)
    psum x1, waiting for transfers between devices, step(): packed = lax.psum(to_sum, FT)  83.1 us
    all_to_all x1, waiting for transfers between devices, step(): lax.all_to_all(spread_res, FT, 0, 0, tiled=True).reshape(count_all, -1)  71.6 us
    all_to_all x1, waiting for transfers between devices, step(): pieces = lax.all_to_all(partial_t, FT, 0, 0, tiled=True)  59.3 us
    all_to_all x1, blocking collectives, step(): grad_own = jnp.sum(lax.all_to_all(pair_sum, YX, 0, 0, tiled=True), axis=0)  24.3 us
    all_to_all x1, waiting for transfers between devices, step(): lax.all_to_all(jnp.broadcast_to(grad_own[None], (n_yx,) + grad_own.shape)...  19 us
    gather x1, local copies, waits for them, and re-layouts, step(): batch_x = jnp.take(dataset, indices, axis=0)  13.7 us
    gather x1, local copies, waits for them, and re-layouts, step(): batch_t = jnp.take(late[0], late[1], axis=0)  11.8 us
    dot_general x2, matrix products, contract(): lax.dot_general(left, right, (((1,), (1,)), ((), ())), preferred_element_...  9.22 us
  transfers between devices with their start and end apart: 7, of which 6 were waited for; matrix products, arithmetic and copies ran while one was open for 9% of the time, Pallas kernels for 0%

profile of v5, /device:TPU:0, one launch (start us, length us, event | category | flops | bytes accessed | tf_op | source)
XLA Modules:
  0.0 377.7 jit_solution(17156656851622508983)
XLA Ops:
  7.2 0.0 copy-start
  7.2 0.0 copy-start.5
  7.2 2.2 broadcast_in_dim.44
  9.4 5.6 %all-to-all-start = ((bf16[16,96,512]{2,1,0:T(8,128)(2,1)}), bf16[16,96,512]{2,1,0:T(8,128)(2,1)S(1)}, u32[]{:S(2)}, u32[]{:S(2)}) async-start(bf16[16,96,512]{2,1,0:T(8,128)(2,1)} %broadcast_in_dim.44), calls=%async_computation | async-start | bytes 3145728 | tf_op jit(solution)/shard_map/all_to_all | solution.py:30
  15.0 0.0 copy-done.5
  15.1 13.7 %gather_fusion = bf16[2048,512]{1,0:T(8,128)(2,1)} fusion(bf16[8192,512]{1,0:T(8,128)(2,1)} %param.5, s32[2048]{0:T(1024)S(1)} %fusion.7), kind=kCustom, calls=%fused_computation | custom fusion | bytes 4202496 | tf_op jit(solution)/shard_map/jit(_take)/gather | solution.py:24
  28.8 8.5 %all-to-all-done = bf16[16,96,512]{2,1,0:T(8,128)(2,1)S(1)} async-done(((bf16[16,96,512]{2,1,0:T(8,128)(2,1)}), bf16[16,96,512]{2,1,0:T(8,128)(2,1)S(1)}, u32[]{:S(2)}, u32[]{:S(2)}) %all-to-all-start) | async-done | bytes 1572896 | tf_op jit(solution)/shard_map/all_to_all | solution.py:30
  37.2 7.8 %convolution_convert_fusion = bf16[2048,1536]{0,1:T(8,128)(2,1)} fusion(bf16[1536,512]{1,0:T(8,128)(2,1)S(1)} %bitcast.32, bf16[2048,512]{1,0:T(8,128)(2,1)} %gather_fusion, pred[2048]{0:T(1024)(128)(4,1)S(1)} %compare_and_fusion), kind=kOutput, calls=%fused_computation.3 | convolution fusion | flops 3225419776 | bytes 9963520 | tf_op jit(solution)/shard_map/dot_general | solution.py:13
  45.0 7.5 %all-to-all-start.1 = ((bf16[8,192,2048]{2,1,0:T(8,128)(2,1)}), bf16[8,192,2048]{2,1,0:T(8,128)(2,1)}, u32[]{:S(2)}, u32[]{:S(2)}) async-start(bf16[8,192,2048]{2,1,0:T(8,128)(2,1)} %bitcast.35), calls=%async_computation.1 | async-start | bytes 12582912 | tf_op jit(solution)/shard_map/all_to_all | solution.py:44
  52.5 0.0 copy-done
  52.5 11.8 %gather_fusion.1 = f32[2048]{0:T(1024)S(1)} fusion(f32[8192]{0:T(1024)S(1)} %copy-done, s32[2048]{0:T(1024)S(1)} %fusion.8), kind=kCustom, calls=%fused_computation.1 | custom fusion | bytes 24576 | tf_op jit(solution)/shard_map/jit(_take)/gather | solution.py:43
  64.3 59.3 %all-to-all-done.1 = bf16[8,192,2048]{2,1,0:T(8,128)(2,1)} async-done(((bf16[8,192,2048]{2,1,0:T(8,128)(2,1)}), bf16[8,192,2048]{2,1,0:T(8,128)(2,1)}, u32[]{:S(2)}, u32[]{:S(2)}) %all-to-all-start.1) | async-done | bytes 6291488 | tf_op jit(solution)/shard_map/all_to_all | solution.py:44
  123.7 4.2 %convert_reduce_fusion = f32[192,2048]{1,0:T(8,128)S(1)} fusion(bf16[8,192,2048]{2,1,0:T(8,128)(2,1)} %all-to-all-done.1), kind=kLoop, calls=%fused_computation.2 | loop fusion | flops 5898240 | bytes 7864320 | tf_op jit(solution)/shard_map/reduce_sum | solution.py:45
  127.8 0.4 subtract_convert_fusion
  128.3 3.5 broadcast_in_dim.51
  131.8 4.8 %all-to-all-start.2 = ((bf16[8,192,2048]{2,1,0:T(8,128)(2,1)}), bf16[8,192,2048]{2,1,0:T(8,128)(2,1)}, u32[]{:S(2)}, u32[]{:S(2)}) async-start(bf16[8,192,2048]{2,1,0:T(8,128)(2,1)} %broadcast_in_dim.51), calls=%async_computation.2 | async-start | bytes 12582912 | tf_op jit(solution)/shard_map/all_to_all | solution.py:48
  136.5 71.6 %all-to-all-done.2 = bf16[8,192,2048]{2,1,0:T(8,128)(2,1)} async-done(((bf16[8,192,2048]{2,1,0:T(8,128)(2,1)}), bf16[8,192,2048]{2,1,0:T(8,128)(2,1)}, u32[]{:S(2)}, u32[]{:S(2)}) %all-to-all-start.2) | async-done | bytes 6291488 | tf_op jit(solution)/shard_map/all_to_all | solution.py:48
  208.2 6.9 %fusion = f32[8,2,96,512]{3,2,1,0:T(8,128)S(1)} fusion(bf16[8,2,96,2048]{3,2,1,0:T(8,128)(2,1)} %bitcast.5, bf16[2048,512]{1,0:T(8,128)(2,1)} %gather_fusion, pred[2048]{0:T(1024)(128)(4,1)S(1)} %compare_and_fusion), kind=kOutput, calls=%fused_computation.7 | convolution fusion | flops 3222274048 | bytes 11536384 | tf_op jit(solution)/shard_map/dot_general | solution.py:53
  215.1 1.6 copy-done.2
  216.7 1.3 dynamic-slice_bitcast_fusion
  218.1 0.0 collective-permute-start
  218.1 3.6 collective-permute-done
  221.7 1.8 bitcast_add_fusion
  223.5 24.3 %all_to_all.25 = f32[8,96,512]{2,1,0:T(8,128)S(1)} all-to-all(f32[8,96,512]{2,1,0:T(8,128)S(1)} %bitcast_add_fusion), channel_id=1, replica_groups=mesh['y'=4,'xl'=2,'c'=2,'xh'=2,'z'=4] {'y','xl'}, dimensions={0} | all-to-all | bytes 3145728 | tf_op jit(solution)/shard_map/all_to_all | solution.py:62
  247.8 0.1 reduce_sum.38
  247.9 1.4 broadcast_in_dim.52
  249.3 3.7 all-to-all-start.4
  253.0 0.0 all-reduce.2.cloned.1.call-start
  253.1 0.4 multiply_reduce_fusion
  253.5 0.1 broadcast_in_dim.45
  253.6 1.4 fusion.16
  255.0 19.0 %all-to-all-done.4 = f32[8,96,512]{2,1,0:T(8,128)S(1)} async-done(((f32[8,96,512]{2,1,0:T(8,128)}), f32[8,96,512]{2,1,0:T(8,128)S(1)}, u32[]{:S(2)}, u32[]{:S(2)}) %all-to-all-start.4) | async-done | bytes 1572896 | tf_op jit(solution)/shard_map/all_to_all | solution.py:63
  274.0 0.0 collective-permute-start.1
  274.1 2.0 pad_maximum_fusion
  276.0 0.0 all-reduce.2.cloned.1.call-update
  276.7 83.1 %all-reduce.2.cloned.1.call-done = f32[97,1536]{1,0:T(8,128)} async-done(((f32[97,1536]{1,0:T(8,128)}), f32[97,1536]{1,0:T(8,128)}) %all-reduce.2.cloned.1.call-update) | async-done | bytes 595984 | tf_op jit(solution)/shard_map/psum | solution.py:49
  359.8 0.8 fusion.15
  360.6 0.1 fusion.9
  360.7 1.4 fusion.13
  362.1 2.7 fusion.2
  364.8 0.0 collective-permute-done.1
  364.8 1.8 select_bitcast_fusion.1
  366.6 0.4 maximum_multiply_fusion
  367.0 0.0 copy-start.3
  367.0 0.0 copy-start.1
  367.0 0.7 bitcast_subtract_fusion
  367.7 0.4 copy-done.3
  368.1 2.8 convolution_multiply_fusion
  (8 shorter events, 0.0 us)
Async XLA Ops:
  7.2 45.4 %copy-start = (f32[8192]{0:T(1024)S(1)}, f32[8192]{0:T(1024)}, u32[]{:S(2)}) copy-start(f32[8192]{0:T(1024)} %param.6) | copy-start | bytes 98308
  7.2 7.9 %copy-start.5 = (s32[2048]{0:T(1024)S(1)}, s32[2048]{0:T(1024)}, u32[]{:S(2)}) copy-start(s32[2048]{0:T(1024)} %param.7) | copy-start | bytes 24580
  9.4 27.8 %all-to-all-start = ((bf16[16,96,512]{2,1,0:T(8,128)(2,1)}), bf16[16,96,512]{2,1,0:T(8,128)(2,1)S(1)}, u32[]{:S(2)}, u32[]{:S(2)}) async-start(bf16[16,96,512]{2,1,0:T(8,128)(2,1)} %broadcast_in_dim.44), calls=%async_computation | async-start | bytes 3145728 | tf_op jit(solution)/shard_map/all_to_all | solution.py:30
  45.0 78.7 %all-to-all-start.1 = ((bf16[8,192,2048]{2,1,0:T(8,128)(2,1)}), bf16[8,192,2048]{2,1,0:T(8,128)(2,1)}, u32[]{:S(2)}, u32[]{:S(2)}) async-start(bf16[8,192,2048]{2,1,0:T(8,128)(2,1)} %bitcast.35), calls=%async_computation.1 | async-start | bytes 12582912 | tf_op jit(solution)/shard_map/all_to_all | solution.py:44
  131.8 76.4 %all-to-all-start.2 = ((bf16[8,192,2048]{2,1,0:T(8,128)(2,1)}), bf16[8,192,2048]{2,1,0:T(8,128)(2,1)}, u32[]{:S(2)}, u32[]{:S(2)}) async-start(bf16[8,192,2048]{2,1,0:T(8,128)(2,1)} %broadcast_in_dim.51), calls=%async_computation.2 | async-start | bytes 12582912 | tf_op jit(solution)/shard_map/all_to_all | solution.py:48
  215.1 1.6 copy-start.2
  218.1 3.6 collective-permute-start
  249.3 4.3 %copy-start.4 = (bf16[96,512]{1,0:T(8,128)(2,1)S(1)}, bf16[96,512]{1,0:T(8,128)(2,1)}, u32[]{:S(2)}) copy-start(bf16[96,512]{1,0:T(8,128)(2,1)} %param.8) | copy-start | bytes 294916
  249.3 24.7 %all-to-all-start.4 = ((f32[8,96,512]{2,1,0:T(8,128)}), f32[8,96,512]{2,1,0:T(8,128)S(1)}, u32[]{:S(2)}, u32[]{:S(2)}) async-start(f32[8,96,512]{2,1,0:T(8,128)} %broadcast_in_dim.52), calls=%async_computation.4 | async-start | bytes 3145728 | tf_op jit(solution)/shard_map/all_to_all | solution.py:63
  253.0 106.8 %all-reduce.2.cloned.1.call-start = ((), (), s32[]{:S(2)}) async-start(), calls=%async_computation.5 | async-start | bytes 1277952 | tf_op jit(solution)/shard_map/psum | solution.py:49
  274.0 90.8 %collective-permute-start.1 = (f32[8,96,512]{2,1,0:T(8,128)S(1)}, f32[8,96,512]{2,1,0:T(8,128)}, u32[]{:S(2)}, u32[]{:S(2)}) collective-permute-start(f32[8,96,512]{2,1,0:T(8,128)S(1)} %all-to-all-done.4), channel_id=1, source_target_pairs={{0,8},{8,0},{1,9},{9,1},{2,10},{10,2},{3,11},{11,3},{4,12},{12,4},... | collective-permute-start | bytes 4718600 | tf_op jit(solution)/shard_map/ppermute | solution.py:66
  367.0 1.1 copy-start.3
  367.0 3.8 %copy-start.1 = (f32[8192]{0:T(1024)S(1)}, f32[8192]{0:T(1024)}, u32[]{:S(2)}) copy-start(f32[8192]{0:T(1024)} %param.6) | copy-start | bytes 98308
Sparse Core Ops, SparseCore 0:
  276.2 83.5 all-reduce.1

commit v6 on v5

--- a/solution.py
+++ b/solution.py
@@ -50,15 +50,19 @@
     inner = packed[:rows_own]
     norms_b = packed[rows_own]
     own_sq = lax.dynamic_slice_in_dim(norms_b, lax.axis_index(DP) * rows_own, rows_own, 0)
-    grad_part = jnp.dot(residual_t, batch_x, preferred_element_type=jnp.float32)
-    width = grad_part.shape[1]
     me_c = lax.axis_index("c")
     swap = [(0, 1), (1, 0)]
-    grad4 = grad_part.reshape(n_yx, n_c, rows_own, width)
-    from_pair = lax.ppermute(
-        lax.dynamic_index_in_dim(grad4, 1 - me_c, 1, keepdims=False), "c", swap
-    )
-    pair_sum = lax.dynamic_index_in_dim(grad4, me_c, 1, keepdims=False) + from_pair
+    width = batch_x.shape[1]
+    res4 = residual_t.reshape(n_yx, n_c, rows_own, -1)
+
+    def grad_half(c):
+        rows = lax.dynamic_index_in_dim(res4, c, 1, keepdims=False).reshape(n_yx * rows_own, -1)
+        grad = jnp.dot(rows, batch_x, preferred_element_type=jnp.float32)
+        return grad.reshape(n_yx, rows_own, width)
+
+    from_pair = lax.ppermute(grad_half(1 - me_c), "c", swap)
+    own_half = lax.optimization_barrier(grad_half(me_c))
+    pair_sum = own_half + from_pair
     grad_own = jnp.sum(lax.all_to_all(pair_sum, YX, 0, 0, tiled=True), axis=0)
     chips = lax.all_to_all(
         jnp.broadcast_to(grad_own[None], (n_yx,) + grad_own.shape), YX, 0, 0, tiled=True

time: 379 us -> 375 us (0.989)
    dot_general x1 -> x2, matrix products: 6.92 us -> 9.96 us  [grad_half(): grad = jnp.dot(rows, batch_x, preferred_element_type=jnp.float32)]
  transfers between devices with their start and end apart: 7 -> 7, of which waited for: 6 -> 5; matrix products, arithmetic and copies ran while one was open for 9% -> 10% of each run, Pallas kernels for 0% -> 0%
where the time goes in v6:
time: 375 us; the launch traced here: 374 us
  waiting for transfers between devices  242 us (65%)
  local copies, waits for them, and re-layouts  33.9 us (9%)
  matrix products  24.7 us (7%)
  blocking collectives  24.7 us (7%)
  starting transfers between devices  21.6 us (6%)
  between operations  14.9 us (4%)
  other arithmetic  11.7 us (3%)
    psum x1, waiting for transfers between devices, step(): packed = lax.psum(to_sum, FT)  83.6 us
    all_to_all x1, waiting for transfers between devices, step(): lax.all_to_all(spread_res, FT, 0, 0, tiled=True).reshape(count_all, -1)  71.6 us
    all_to_all x1, waiting for transfers between devices, step(): pieces = lax.all_to_all(partial_t, FT, 0, 0, tiled=True)  59.3 us
    all_to_all x1, blocking collectives, step(): grad_own = jnp.sum(lax.all_to_all(pair_sum, YX, 0, 0, tiled=True), axis=0)  24.7 us
    all_to_all x1, waiting for transfers between devices, step(): lax.all_to_all(jnp.broadcast_to(grad_own[None], (n_yx,) + grad_own.shape)...  19.2 us
    gather x1, local copies, waits for them, and re-layouts, step(): batch_x = jnp.take(dataset, indices, axis=0)  13.7 us
    gather x1, local copies, waits for them, and re-layouts, step(): batch_t = jnp.take(late[0], late[1], axis=0)  11.8 us
    dot_general x2, matrix products, grad_half(): grad = jnp.dot(rows, batch_x, preferred_element_type=jnp.float32)  9.96 us
  transfers between devices with their start and end apart: 7, of which 5 were waited for; matrix products, arithmetic and copies ran while one was open for 10% of the time, Pallas kernels for 0%

profile of v6, /device:TPU:0, one launch (start us, length us, event | category | flops | bytes accessed | tf_op | source)
XLA Modules:
  0.0 373.8 jit_solution(2329386748825385926)
XLA Ops:
  7.2 0.0 copy-start
  7.2 0.0 copy-start.3
  7.2 2.2 broadcast_in_dim.44
  9.4 5.6 %all-to-all-start = ((bf16[16,96,512]{2,1,0:T(8,128)(2,1)}), bf16[16,96,512]{2,1,0:T(8,128)(2,1)S(1)}, u32[]{:S(2)}, u32[]{:S(2)}) async-start(bf16[16,96,512]{2,1,0:T(8,128)(2,1)} %broadcast_in_dim.44), calls=%async_computation | async-start | bytes 3145728 | tf_op jit(solution)/shard_map/all_to_all | solution.py:30
  15.0 0.0 copy-done.3
  15.0 13.7 %gather_fusion = bf16[2048,512]{1,0:T(8,128)(2,1)} fusion(bf16[8192,512]{1,0:T(8,128)(2,1)} %param.5, s32[2048]{0:T(1024)S(1)} %fusion.13), kind=kCustom, calls=%fused_computation | custom fusion | bytes 4202496 | tf_op jit(solution)/shard_map/jit(_take)/gather | solution.py:24
  28.8 8.5 %all-to-all-done = bf16[16,96,512]{2,1,0:T(8,128)(2,1)S(1)} async-done(((bf16[16,96,512]{2,1,0:T(8,128)(2,1)}), bf16[16,96,512]{2,1,0:T(8,128)(2,1)S(1)}, u32[]{:S(2)}, u32[]{:S(2)}) %all-to-all-start) | async-done | bytes 1572896 | tf_op jit(solution)/shard_map/all_to_all | solution.py:30
  37.2 7.8 %convolution_convert_fusion = bf16[2048,1536]{0,1:T(8,128)(2,1)} fusion(bf16[1536,512]{1,0:T(8,128)(2,1)S(1)} %bitcast.33, bf16[2048,512]{1,0:T(8,128)(2,1)} %gather_fusion, pred[2048]{0:T(1024)(128)(4,1)S(1)} %compare_and_fusion), kind=kOutput, calls=%fused_computation.3 | convolution fusion | flops 3225419776 | bytes 9963520 | tf_op jit(solution)/shard_map/dot_general | solution.py:13
  45.0 7.5 %all-to-all-start.1 = ((bf16[8,192,2048]{2,1,0:T(8,128)(2,1)}), bf16[8,192,2048]{2,1,0:T(8,128)(2,1)}, u32[]{:S(2)}, u32[]{:S(2)}) async-start(bf16[8,192,2048]{2,1,0:T(8,128)(2,1)} %bitcast.36), calls=%async_computation.1 | async-start | bytes 12582912 | tf_op jit(solution)/shard_map/all_to_all | solution.py:44
  52.5 0.0 copy-done
  52.5 11.8 %gather_fusion.1 = f32[2048]{0:T(1024)S(1)} fusion(f32[8192]{0:T(1024)S(1)} %copy-done, s32[2048]{0:T(1024)S(1)} %fusion.14), kind=kCustom, calls=%fused_computation.1 | custom fusion | bytes 24576 | tf_op jit(solution)/shard_map/jit(_take)/gather | solution.py:43
  64.3 59.3 %all-to-all-done.1 = bf16[8,192,2048]{2,1,0:T(8,128)(2,1)} async-done(((bf16[8,192,2048]{2,1,0:T(8,128)(2,1)}), bf16[8,192,2048]{2,1,0:T(8,128)(2,1)}, u32[]{:S(2)}, u32[]{:S(2)}) %all-to-all-start.1) | async-done | bytes 6291488 | tf_op jit(solution)/shard_map/all_to_all | solution.py:44
  123.7 4.2 %convert_reduce_fusion = f32[192,2048]{1,0:T(8,128)S(1)} fusion(bf16[8,192,2048]{2,1,0:T(8,128)(2,1)} %all-to-all-done.1), kind=kLoop, calls=%fused_computation.2 | loop fusion | flops 5898240 | bytes 7864320 | tf_op jit(solution)/shard_map/reduce_sum | solution.py:45
  127.8 0.4 subtract_convert_fusion
  128.3 3.5 broadcast_in_dim.51
  131.8 4.8 %all-to-all-start.2 = ((bf16[8,192,2048]{2,1,0:T(8,128)(2,1)}), bf16[8,192,2048]{2,1,0:T(8,128)(2,1)}, u32[]{:S(2)}, u32[]{:S(2)}) async-start(bf16[8,192,2048]{2,1,0:T(8,128)(2,1)} %broadcast_in_dim.51), calls=%async_computation.2 | async-start | bytes 12582912 | tf_op jit(solution)/shard_map/all_to_all | solution.py:48
  136.5 71.6 %all-to-all-done.2 = bf16[8,192,2048]{2,1,0:T(8,128)(2,1)} async-done(((bf16[8,192,2048]{2,1,0:T(8,128)(2,1)}), bf16[8,192,2048]{2,1,0:T(8,128)(2,1)}, u32[]{:S(2)}, u32[]{:S(2)}) %all-to-all-start.2) | async-done | bytes 6291488 | tf_op jit(solution)/shard_map/all_to_all | solution.py:48
  208.2 5.6 %fusion = f32[8,96,512]{2,1,0:T(8,128)} fusion(bf16[8,2,96,2048]{3,2,1,0:T(8,128)(2,1)} %bitcast.5, s32[]{:T(128)S(6)} %select_n.48, bf16[2048,512]{1,0:T(8,128)(2,1)} %gather_fusion, pred[2048]{0:T(1024)(128)(4,1)S(1)} %compare_and_fusion), kind=kOutput, calls=%fused_computation.6 | convolution fusion | flops 1611661312 | bytes 6817796 | tf_op jit(solution)/shard_map/dot_general | solution.py:60
  213.7 0.0 collective-permute-start
  213.7 4.4 %fusion.2 = f32[8,96,512]{2,1,0:T(8,128)S(1)} fusion(bf16[8,2,96,2048]{3,2,1,0:T(8,128)(2,1)} %bitcast.5, s32[]{:T(128)S(6)} %select_n.47, bf16[2048,512]{1,0:T(8,128)(2,1)} %gather_fusion, pred[2048]{0:T(1024)(128)(4,1)S(1)} %compare_and_fusion), kind=kOutput, calls=%fused_computation.8 | convolution fusion | flops 1611661312 | bytes 6817796 | tf_op jit(solution)/shard_map/dot_general | solution.py:60
  218.1 0.0 collective-permute-done
  218.2 0.3 add.74
  218.5 24.7 %all_to_all.25 = f32[8,96,512]{2,1,0:T(8,128)S(1)} all-to-all(f32[8,96,512]{2,1,0:T(8,128)S(1)} %add.74), channel_id=1, replica_groups=mesh['y'=4,'xl'=2,'c'=2,'xh'=2,'z'=4] {'y','xl'}, dimensions={0} | all-to-all | bytes 3145728 | tf_op jit(solution)/shard_map/all_to_all | solution.py:66
  243.2 0.1 reduce_sum.38
  243.3 1.4 broadcast_in_dim.52
  244.7 0.0 copy-start.2
  244.7 3.7 all-to-all-start.4
  248.4 0.0 all-reduce.2.cloned.1.call-start
  248.5 0.4 multiply_reduce_fusion
  248.9 0.1 broadcast_in_dim.45
  249.0 0.0 copy-done.2
  249.0 1.4 fusion.22
  250.4 19.2 %all-to-all-done.4 = f32[8,96,512]{2,1,0:T(8,128)S(1)} async-done(((f32[8,96,512]{2,1,0:T(8,128)}), f32[8,96,512]{2,1,0:T(8,128)S(1)}, u32[]{:S(2)}, u32[]{:S(2)}) %all-to-all-start.4) | async-done | bytes 1572896 | tf_op jit(solution)/shard_map/all_to_all | solution.py:67
  269.6 0.0 collective-permute-start.1
  269.6 2.0 pad_maximum_fusion
  271.6 0.0 all-reduce.2.cloned.1.call-update
  272.3 83.6 %all-reduce.2.cloned.1.call-done = f32[97,1536]{1,0:T(8,128)} async-done(((f32[97,1536]{1,0:T(8,128)}), f32[97,1536]{1,0:T(8,128)}) %all-reduce.2.cloned.1.call-update) | async-done | bytes 595984 | tf_op jit(solution)/shard_map/psum | solution.py:49
  355.9 0.8 fusion.21
  356.7 0.1 fusion.17
  356.8 1.4 fusion.19
  358.2 2.7 fusion.8
  360.9 0.0 collective-permute-done.1
  360.9 1.8 select_bitcast_fusion.1
  362.7 0.4 maximum_multiply_fusion
  363.1 0.0 copy-start.1
  363.1 0.7 bitcast_subtract_fusion
  363.8 0.4 copy-done.1
  364.1 2.8 convolution_multiply_fusion
  (4 shorter events, 0.0 us)
Async XLA Ops:
  7.2 45.4 %copy-start = (f32[8192]{0:T(1024)S(1)}, f32[8192]{0:T(1024)}, u32[]{:S(2)}) copy-start(f32[8192]{0:T(1024)} %param.6) | copy-start | bytes 98308
  7.2 7.8 %copy-start.3 = (s32[2048]{0:T(1024)S(1)}, s32[2048]{0:T(1024)}, u32[]{:S(2)}) copy-start(s32[2048]{0:T(1024)} %param.7) | copy-start | bytes 24580
  9.4 27.8 %all-to-all-start = ((bf16[16,96,512]{2,1,0:T(8,128)(2,1)}), bf16[16,96,512]{2,1,0:T(8,128)(2,1)S(1)}, u32[]{:S(2)}, u32[]{:S(2)}) async-start(bf16[16,96,512]{2,1,0:T(8,128)(2,1)} %broadcast_in_dim.44), calls=%async_computation | async-start | bytes 3145728 | tf_op jit(solution)/shard_map/all_to_all | solution.py:30
  45.0 78.6 %all-to-all-start.1 = ((bf16[8,192,2048]{2,1,0:T(8,128)(2,1)}), bf16[8,192,2048]{2,1,0:T(8,128)(2,1)}, u32[]{:S(2)}, u32[]{:S(2)}) async-start(bf16[8,192,2048]{2,1,0:T(8,128)(2,1)} %bitcast.36), calls=%async_computation.1 | async-start | bytes 12582912 | tf_op jit(solution)/shard_map/all_to_all | solution.py:44
  131.8 76.4 %all-to-all-start.2 = ((bf16[8,192,2048]{2,1,0:T(8,128)(2,1)}), bf16[8,192,2048]{2,1,0:T(8,128)(2,1)}, u32[]{:S(2)}, u32[]{:S(2)}) async-start(bf16[8,192,2048]{2,1,0:T(8,128)(2,1)} %broadcast_in_dim.51), calls=%async_computation.2 | async-start | bytes 12582912 | tf_op jit(solution)/shard_map/all_to_all | solution.py:48
  213.7 4.4 %collective-permute-start = (f32[8,96,512]{2,1,0:T(8,128)}, f32[8,96,512]{2,1,0:T(8,128)S(1)}, u32[]{:S(2)}, u32[]{:S(2)}) collective-permute-start(f32[8,96,512]{2,1,0:T(8,128)} %fusion), channel_id=1, source_target_pairs={{0,8},{8,0},{1,9},{9,1},{2,10},{10,2},{3,11},{11,3},{4,12},{12,4},... | collective-permute-start | bytes 4718600 | tf_op jit(solution)/shard_map/ppermute | solution.py:63
  244.7 4.3 %copy-start.2 = (bf16[96,512]{1,0:T(8,128)(2,1)S(1)}, bf16[96,512]{1,0:T(8,128)(2,1)}, u32[]{:S(2)}) copy-start(bf16[96,512]{1,0:T(8,128)(2,1)} %param.8) | copy-start | bytes 294916
  244.7 24.9 %all-to-all-start.4 = ((f32[8,96,512]{2,1,0:T(8,128)}), f32[8,96,512]{2,1,0:T(8,128)S(1)}, u32[]{:S(2)}, u32[]{:S(2)}) async-start(f32[8,96,512]{2,1,0:T(8,128)} %broadcast_in_dim.52), calls=%async_computation.4 | async-start | bytes 3145728 | tf_op jit(solution)/shard_map/all_to_all | solution.py:67
  248.4 107.5 %all-reduce.2.cloned.1.call-start = ((), (), s32[]{:S(2)}) async-start(), calls=%async_computation.5 | async-start | bytes 1277952 | tf_op jit(solution)/shard_map/psum | solution.py:49
  269.6 91.3 %collective-permute-start.1 = (f32[8,96,512]{2,1,0:T(8,128)S(1)}, f32[8,96,512]{2,1,0:T(8,128)}, u32[]{:S(2)}, u32[]{:S(2)}) collective-permute-start(f32[8,96,512]{2,1,0:T(8,128)S(1)} %all-to-all-done.4), channel_id=1, source_target_pairs={{0,8},{8,0},{1,9},{9,1},{2,10},{10,2},{3,11},{11,3},{4,12},{12,4},... | collective-permute-start | bytes 4718600 | tf_op jit(solution)/shard_map/ppermute | solution.py:70
  363.1 1.1 copy-start.1
Sparse Core Ops, SparseCore 0:
  271.7 84.0 all-reduce.1
